TPU v7x, 512 devices: a whole 4x8x8 slice. The times are simulated.
512 devices in a mesh: dp: 32 (over x, z), mp: 16 (over y, core).
Axes of the slice: x: 4, y: 8, z: 8, core: 2. Of those that a mesh axis runs over, the one named last changes fastest.
Arguments:
- hidden_rows: bfloat16 [16384, 8192], P('dp', 'mp'), may hold values from -6 to 6
- base_weight: bfloat16 [8192, 4096], P('mp'), may hold values from -0.0625 to 0.0625
- adapter_down: bfloat16 [32, 64, 8192], P('dp', None, 'mp'), may hold values from -0.0625 to 0.0625
- adapter_up: bfloat16 [32, 64, 4096], P('dp', None, 'mp'), may hold values from -0.75 to 0.75
- adapter_of_row: int32 [16384, 1], P('dp'), may hold values from 0 to 31; in each aligned block of 512 rows (0 to 511, 512 to 1023, ...) at most 32 rows name the same one
- holder_map: int32 [32], replicated, may hold values from 0 to 31, each once
Outputs:
- projected: bfloat16 [16384, 4096], P('dp', 'mp')
Inputs may be any that keep to these rules, and one draw needn't show every extreme that they name: `adapter_of_row`: within the 512 rows of one index of dp (aligned blocks), no adapter is named by more than 32 rows; every adapter is named by some row. `holder_map`: each of the 32 slots holds exactly one adapter.
All inputs are finite; a program needn't handle non-finite values.
Results may differ from a plain program's by a relative error of at most 0.02.
Values may be sent and summed in bfloat16 or wider, within the bound.
No kernel may reach another device: no remote copies, remote signals or barrier semaphores. Data moves between devices by JAX's collectives and lax.ppermute only.
A program may use at most 64 MiB of HBM per device.

v0:
```python
import jax
import jax.numpy as jnp
from jax import lax
from jax.sharding import PartitionSpec as P


def per_device(hidden_rows, base_weight, adapter_down, adapter_up, adapter_of_row, holder_map):
    row_count, feat_width = hidden_rows.shape
    holders = lax.axis_size("dp")
    capacity = 2 * row_count // holders
    adapter_ids = adapter_of_row[:, 0]
    matches = adapter_ids[:, None] == jnp.arange(holder_map.shape[0], dtype=jnp.int32)[None, :]
    slot_of_row = jnp.sum(jnp.where(matches, holder_map[None, :], 0), axis=1)
    members = (slot_of_row[:, None] == jnp.arange(holders, dtype=jnp.int32)[None, :]).astype(
        jnp.int32
    )
    earlier = jnp.cumsum(members, axis=0) - members
    position = jnp.sum(earlier * members, axis=1)
    destination = slot_of_row * capacity + position
    packed = (
        jnp.zeros((holders * capacity, feat_width), jnp.bfloat16).at[destination].set(hidden_rows)
    )
    packed = packed.reshape(holders, capacity, feat_width)
    base_terms = jnp.dot(hidden_rows, base_weight, preferred_element_type=jnp.float32)
    base_total = lax.psum_scatter(
        base_terms.astype(jnp.bfloat16), "mp", scatter_dimension=1, tiled=True
    ).astype(jnp.float32)
    section = packed
    partial_value = jnp.einsum(
        "hcf,hkf->hck",
        section,
        lax.all_gather(adapter_down, "dp", axis=0, tiled=True),
        preferred_element_type=jnp.float32,
    )
    reduced = lax.psum(partial_value.astype(jnp.bfloat16), "mp")
    section = reduced
    buckets = jnp.einsum(
        "hck,hko->hco",
        section,
        lax.all_gather(adapter_up, "dp", axis=0, tiled=True),
        preferred_element_type=jnp.float32,
    ).astype(jnp.bfloat16)
    adapter_out = buckets.reshape(holders * capacity, buckets.shape[2])[destination]
    return (base_total + adapter_out.astype(jnp.float32)).astype(jnp.bfloat16)


def solution(mesh):
    placed = (
        P("dp", "mp"),
        P("mp", None),
        P("dp", None, "mp"),
        P("dp", None, "mp"),
        P("dp", None),
        P(),
    )
    return jax.shard_map(
        per_device, mesh=mesh, in_specs=placed, out_specs=P("dp", "mp"), check_vma=False
    )
```

profile of v0, /device:TPU:1, one launch (start us, length us, event | category | flops | bytes accessed | tf_op | source)
XLA Modules:
  0.0 371.0 jit_solution(2252982581453105532)
XLA Ops:
  6.5 0.0 copy-start
  6.5 0.0 all-gather.3.cloned.1.call-start
  6.5 0.7 all-gather.3.cloned.1.call-update
  7.3 0.0 all-gather.5.cloned.1.call-start
  7.3 0.7 all-gather.5.cloned.1.call-update
  8.0 0.0 all-reduce.2.cloned.1.call-start
  8.1 0.8 select_reduce_fusion
  8.9 1.2 reduce-window.6
  10.0 0.2 slice_reduce_fusion
  10.3 0.1 fusion.4
  10.4 3.2 scatter_custom_fusion
  13.6 82.4 %all-gather.3.cloned.1.call-done = bf16[32,64,512]{2,1,0:T(8,128)(2,1)} async-done(((bf16[1,64,512]{2,1,0:T(8,128)(2,1)}), bf16[32,64,512]{2,1,0:T(8,128)(2,1)}) %all-gather.3.cloned.1.call-update) | async-done | bytes 2097168 | tf_op jit(solution)/shard_map/all_gather | solution.py:32
  96.0 3.0 convolution_convert_fusion.2
  99.0 0.0 all-reduce.2.cloned.1.call-update
  99.0 0.0 reduce-scatter.2.cloned.1.call-start
  99.1 0.0 copy-done
  99.1 6.5 %convolution_convert_fusion = bf16[512,4096]{1,0:T(8,128)(2,1)} fusion(bf16[512,512]{1,0:T(8,128)(2,1)S(1)} %copy-done, bf16[512,4096]{1,0:T(8,128)(2,1)} %param.7), kind=kOutput, calls=%fused_computation.2 | convolution fusion | flops 2149580800 | bytes 8912896 | tf_op jit(solution)/shard_map/dot_general | solution.py:24
  105.6 0.0 reduce-scatter.2.cloned.1.call-update
  105.7 72.2 %all-gather.5.cloned.1.call-done = bf16[32,64,256]{2,1,0:T(8,128)(2,1)} async-done(((bf16[1,64,256]{2,1,0:T(8,128)(2,1)}), bf16[32,64,256]{2,1,0:T(8,128)(2,1)}) %all-gather.5.cloned.1.call-update) | async-done | bytes 1048592 | tf_op jit(solution)/shard_map/all_gather | solution.py:40
  177.8 117.8 %all-reduce.2.cloned.1.call-done = bf16[32,32,64]{2,1,0:T(8,128)(2,1)} async-done(((bf16[32,32,64]{2,1,0:T(8,128)(2,1)}), bf16[32,32,64]{2,1,0:T(8,128)(2,1)}) %all-reduce.2.cloned.1.call-update) | async-done | bytes 131088 | tf_op jit(solution)/shard_map/psum | solution.py:35
  295.7 1.6 convolution_convert_fusion.1
  297.3 2.0 gather_fusion
  299.2 63.5 %reduce-scatter.2.cloned.1.call-done = bf16[512,256]{1,0:T(8,128)(2,1)} async-done(((bf16[512,4096]{1,0:T(8,128)(2,1)}), bf16[512,256]{1,0:T(8,128)(2,1)}) %reduce-scatter.2.cloned.1.call-update) | async-done | bytes 262160 | tf_op jit(solution)/shard_map/reduce_scatter | solution.py:25
  362.7 1.7 add_convert_fusion
  (6 shorter events, 0.1 us)
Async XLA Ops:
  6.5 92.5 %copy-start = (bf16[512,512]{1,0:T(8,128)(2,1)S(1)}, bf16[512,512]{1,0:T(8,128)(2,1)}, u32[]{:S(2)}) copy-start(bf16[512,512]{1,0:T(8,128)(2,1)} %param.6) | copy-start | bytes 1572868
  6.5 89.5 %all-gather.3.cloned.1.call-start = ((), (), s32[]{:S(2)}) async-start(), calls=%async_computation.2 | async-start | bytes 2162688 | tf_op jit(solution)/shard_map/all_gather | solution.py:32
  7.3 170.6 %all-gather.5.cloned.1.call-start = ((), (), s32[]{:S(2)}) async-start(), calls=%async_computation.4 | async-start | bytes 1081344 | tf_op jit(solution)/shard_map/all_gather | solution.py:40
  8.0 287.7 %all-reduce.2.cloned.1.call-start = ((), (), s32[]{:S(2)}) async-start(), calls=%async_computation.3 | async-start | bytes 524288 | tf_op jit(solution)/shard_map/psum | solution.py:35
  99.0 263.7 %reduce-scatter.2.cloned.1.call-start = ((), (), s32[]{:S(2)}) async-start(), calls=%async_computation.1 | async-start | bytes 4456448 | tf_op jit(solution)/shard_map/reduce_scatter | solution.py:25
Sparse Core Ops, SparseCore 0:
  10.5 85.4 all-gather.2
  99.2 78.5 all-gather.4
  180.2 115.4 all-reduce.1
  298.6 64.0 reduce-scatter.1
where the time goes:
time: 372 us; the launch traced here: 371 us
  waiting for transfers between devices  337 us (91%)
  between operations  13.2 us (4%)
  matrix products  11.1 us (3%)
  local copies, waits for them, and re-layouts  5.4 us (1%)
  other arithmetic  3.85 us (1%)
    psum x1, waiting for transfers between devices, per_device(): reduced = lax.psum(partial_value.astype(jnp.bfloat16), 'mp')  118 us
    all_gather x1, waiting for transfers between devices, per_device(): lax.all_gather(adapter_down, 'dp', axis=0, tiled=True)  82.4 us
    all_gather x1, waiting for transfers between devices, per_device(): lax.all_gather(adapter_up, 'dp', axis=0, tiled=True)  72.2 us
    reduce_scatter x1, waiting for transfers between devices, per_device(): lax.psum_scatter(base_terms.astype(jnp.bfloat16), 'mp', scatter_dimension...  63.5 us
  transfers between devices with their start and end apart: 4, of which 4 were waited for; matrix products, arithmetic and copies ran while one was open for 5% of the time, Pallas kernels for 0%

commit v1 on v0

v1 whole, which is shorter than its diff:
```python
import jax
import jax.numpy as jnp
from jax import lax
from jax.sharding import PartitionSpec as P


def per_device(hidden_rows, base_weight, adapter_down, adapter_up, adapter_of_row, holder_map):
    row_count, feat_width = hidden_rows.shape
    holders = lax.axis_size("dp")
    n_mp = lax.axis_size("mp")
    rank = adapter_down.shape[1]
    out_width = adapter_up.shape[2]
    adapters = holder_map.shape[0]

    adapter_ids = adapter_of_row[:, 0]
    matches = adapter_ids[:, None] == jnp.arange(adapters, dtype=jnp.int32)[None, :]
    slot_of_row = jnp.sum(jnp.where(matches, holder_map[None, :], 0), axis=1)
    slot_hot = slot_of_row[:, None] == jnp.arange(holders, dtype=jnp.int32)[None, :]

    both = jnp.concatenate([adapter_down[0], adapter_up[0]], axis=1)
    stack = lax.all_gather(both, "dp", axis=0, tiled=False)
    down_w = stack[:, :, :feat_width]
    up_w = stack[:, :, feat_width:]

    base_terms = jnp.dot(hidden_rows, base_weight, preferred_element_type=jnp.float32)
    base_bf = base_terms.astype(jnp.bfloat16)
    base_bf, stack = lax.optimization_barrier((base_bf, stack))
    base_total = lax.psum_scatter(base_bf, "mp", scatter_dimension=1, tiled=True).astype(
        jnp.float32
    )

    every = jnp.dot(
        hidden_rows,
        down_w.transpose(2, 0, 1).reshape(feat_width, holders * rank),
        preferred_element_type=jnp.float32,
    ).reshape(row_count, holders, rank)
    partial_down = jnp.sum(jnp.where(slot_hot[:, :, None], every, 0.0), axis=1)
    spread = jnp.broadcast_to(partial_down.astype(jnp.bfloat16)[None], (n_mp, row_count, rank))
    gathered = lax.all_to_all(spread, "mp", 0, 0, tiled=False)
    down = jnp.sum(gathered.astype(jnp.float32), axis=0).astype(jnp.bfloat16)

    placed = jnp.where(slot_hot[:, :, None], down[:, None, :], jnp.zeros((), jnp.bfloat16))
    lift = jnp.dot(
        placed.reshape(row_count, holders * rank),
        up_w.reshape(holders * rank, out_width),
        preferred_element_type=jnp.float32,
    ).astype(jnp.bfloat16)
    return (base_total + lift.astype(jnp.float32)).astype(jnp.bfloat16)


def solution(mesh):
    placed = (
        P("dp", "mp"),
        P("mp", None),
        P("dp", None, "mp"),
        P("dp", None, "mp"),
        P("dp", None),
        P(),
    )
    return jax.shard_map(
        per_device, mesh=mesh, in_specs=placed, out_specs=P("dp", "mp"), check_vma=False
    )
```

time: 372 us -> 192 us (0.52)
  waiting for transfers between devices: 337 us -> 116 us
  blocking collectives: 0 us -> 45.1 us
    psum x1 -> x0, waiting for transfers between devices: 118 us -> none  [per_device(): reduced = lax.psum(partial_value.astype(jnp.bfloat16), 'mp')]
    all_gather x2 -> x1, waiting for transfers between devices: 155 us -> 83.4 us  [per_device(): stack = lax.all_gather(both, 'dp', axis=0, tiled=False)]
    all_to_all x0 -> x1, blocking collectives: none -> 45.1 us  [per_device(): gathered = lax.all_to_all(spread, 'mp', 0, 0, tiled=False)]
    reduce_scatter x1, waiting for transfers between devices: 63.5 us -> 32.5 us  [per_device(): lax.psum_scatter(base_bf, 'mp', scatter_dimension=1, tiled=True)]
  transfers between devices with their start and end apart: 4 -> 2, of which waited for: 4 -> 2; matrix products, arithmetic and copies ran while one was open for 5% -> 6% of each run, Pallas kernels for 0% -> 0%
where the time goes in v1:
time: 192 us; the launch traced here: 189 us
  waiting for transfers between devices  116 us (60%)
  blocking collectives  45.1 us (23%)
  between operations  13.5 us (7%)
  matrix products  10.5 us (5%)
  other arithmetic  2.45 us (1%)
    all_gather x1, waiting for transfers between devices, per_device(): stack = lax.all_gather(both, 'dp', axis=0, tiled=False)  83.4 us
    all_to_all x1, blocking collectives, per_device(): gathered = lax.all_to_all(spread, 'mp', 0, 0, tiled=False)  45.1 us
    reduce_scatter x1, waiting for transfers between devices, per_device(): lax.psum_scatter(base_bf, 'mp', scatter_dimension=1, tiled=True)  32.5 us
    dot_general x1, matrix products, per_device(): jnp.dot(hidden_rows, base_weight, preferred_element_type=jnp.float32)  6.47 us
  transfers between devices with their start and end apart: 2, of which 2 were waited for; matrix products, arithmetic and copies ran while one was open for 6% of the time, Pallas kernels for 0%

profile of v1, /device:TPU:1, one launch (start us, length us, event | category | flops | bytes accessed | tf_op | source)
XLA Modules:
  0.0 189.2 jit_solution(6804145400877896313)
XLA Ops:
  6.5 0.0 copy-start
  6.5 0.0 all-gather.3.cloned.1.call-start
  6.5 1.6 pad_maximum_fusion
  8.1 0.0 all-gather.3.cloned.1.call-update
  8.1 0.0 reduce-scatter.2.cloned.1.call-start
  8.2 0.0 copy-done
  8.2 6.5 %convolution_convert_fusion = bf16[512,4096]{1,0:T(8,128)(2,1)} fusion(bf16[512,512]{1,0:T(8,128)(2,1)S(1)} %copy-done, bf16[512,4096]{1,0:T(8,128)(2,1)} %param.7), kind=kOutput, calls=%fused_computation | convolution fusion | flops 2149580800 | bytes 8912896 | tf_op jit(solution)/shard_map/dot_general | solution.py:25
  14.7 0.0 copy-start.1
  14.7 0.0 copy-start.2
  14.7 83.4 %all-gather.3.cloned.1.call-done = bf16[2048,768]{1,0:T(8,128)(2,1)} async-done(((bf16[64,768]{1,0:T(8,128)(2,1)}), bf16[2048,768]{1,0:T(8,128)(2,1)}) %all-gather.3.cloned.1.call-update) | async-done | bytes 3145744 | tf_op jit(solution)/shard_map/all_gather | solution.py:21
  98.0 0.0 reduce-scatter.2.cloned.1.call-update
  98.0 0.0 copy-done.1
  98.1 0.0 copy-done.2
  98.1 0.1 select_reduce_fusion.1
  98.2 1.7 slice.8
  99.9 1.3 fusion.22
  101.2 0.6 select_reduce_fusion
  101.8 0.1 broadcast_in_dim.59
  101.9 45.1 %all_to_all.5 = bf16[16,512,64]{1,2,0:T(8,128)(2,1)S(1)} all-to-all(bf16[16,512,64]{1,2,0:T(8,128)(2,1)S(1)} %broadcast_in_dim.59), channel_id=1, replica_groups=mesh['dp'=32,'mp'=16] {'mp'}, dimensions={0} | all-to-all | bytes 2097152 | tf_op jit(solution)/shard_map/all_to_all | solution.py:39
  147.0 0.1 reduce_sum.32
  147.2 32.5 %reduce-scatter.2.cloned.1.call-done = bf16[512,256]{1,0:T(8,128)(2,1)} async-done(((bf16[512,4096]{1,0:T(8,128)(2,1)}), bf16[512,256]{1,0:T(8,128)(2,1)}) %reduce-scatter.2.cloned.1.call-update) | async-done | bytes 262160 | tf_op jit(solution)/shard_map/reduce_scatter | solution.py:28
  179.6 2.8 %fusion.15 = bf16[512,256]{1,0:T(8,128)(2,1)} fusion(pred[512,32]{0,1:T(8,128)(4,1)S(1)} %iota_compare_fusion, bf16[32,64,768]{2,1,0:T(8,128)(2,1)} %bitcast.27, bf16[512,64]{0,1:T(8,128)(2,1)S(1)} %reduce_sum.32, bf16[512,256]{1,0:T(8,128)(2,1)} %reduce-scatter.2.cloned.1.call-done), kind=kOutput, calls=%fused_computation.9 | convolution fusion | flops 538574848 | bytes 1654784 | tf_op jit(solution)/shard_map/dot_general | solution.py:43
  (1 shorter events, 0.0 us)
Async XLA Ops:
  6.5 1.6 copy-start
  6.5 91.5 %all-gather.3.cloned.1.call-start = ((), (), s32[]{:S(2)}) async-start(), calls=%async_computation.3 | async-start | bytes 3244032 | tf_op jit(solution)/shard_map/all_gather | solution.py:21
  8.1 171.5 %reduce-scatter.2.cloned.1.call-start = ((), (), s32[]{:S(2)}) async-start(), calls=%async_computation.2 | async-start | bytes 4456448 | tf_op jit(solution)/shard_map/reduce_scatter | solution.py:28
  14.7 83.4 %copy-start.1 = (s32[512,1]{0,1:T(1,128)S(1)}, s32[512,1]{0,1:T(1,128)}, u32[]{:S(2)}) copy-start(s32[512,1]{0,1:T(1,128)} %param.10) | copy-start | bytes 6148
  14.7 83.4 %copy-start.2 = (s32[32]{0:T(128)S(1)}, s32[32]{0:T(128)}, u32[]{:S(2)}) copy-start(s32[32]{0:T(128)} %param.11) | copy-start | bytes 388
Sparse Core Ops, SparseCore 0:
  10.5 87.4 all-gather.2
  100.9 78.7 reduce-scatter.1

commit v2 on v1

--- a/solution.py
+++ b/solution.py
@@ -17,17 +17,18 @@
     slot_of_row = jnp.sum(jnp.where(matches, holder_map[None, :], 0), axis=1)
     slot_hot = slot_of_row[:, None] == jnp.arange(holders, dtype=jnp.int32)[None, :]
 
-    both = jnp.concatenate([adapter_down[0], adapter_up[0]], axis=1)
-    stack = lax.all_gather(both, "dp", axis=0, tiled=False)
-    down_w = stack[:, :, :feat_width]
-    up_w = stack[:, :, feat_width:]
-
     base_terms = jnp.dot(hidden_rows, base_weight, preferred_element_type=jnp.float32)
     base_bf = base_terms.astype(jnp.bfloat16)
-    base_bf, stack = lax.optimization_barrier((base_bf, stack))
     base_total = lax.psum_scatter(base_bf, "mp", scatter_dimension=1, tiled=True).astype(
         jnp.float32
     )
+
+    both = jnp.concatenate([adapter_down[0], adapter_up[0]], axis=1)
+    base_bf, both = lax.optimization_barrier((base_bf, both))
+    spread_w = jnp.broadcast_to(both[None], (holders,) + both.shape)
+    stack = lax.all_to_all(spread_w, "dp", 0, 0, tiled=False)
+    down_w = stack[:, :, :feat_width]
+    up_w = stack[:, :, feat_width:]
 
     every = jnp.dot(
         hidden_rows,

time: 192 us -> 155 us (0.81); the launches traced: 189 us -> 155 us
  waiting for transfers between devices: 116 us -> 71.3 us
  starting transfers between devices: 0.04 us -> 14 us
  blocking collectives: 45.1 us -> 39.6 us
  local copies, waits for them, and re-layouts: 1.83 us -> 4.07 us
    all_gather x1 -> x0, waiting for transfers between devices: 83.4 us -> none  [per_device(): stack = lax.all_gather(both, 'dp', axis=0, tiled=False)]
    all_to_all x0 -> x1, waiting for transfers between devices: none -> 70.6 us  [per_device(): stack = lax.all_to_all(spread_w, 'dp', 0, 0, tiled=False)]
    reduce_scatter x1, waiting for transfers between devices: 32.5 us -> 0.02 us  [per_device(): lax.psum_scatter(base_bf, 'mp', scatter_dimension=1, tiled=True)]
    all_to_all x0 -> x1, starting transfers between devices: none -> 14 us  [per_device(): stack = lax.all_to_all(spread_w, 'dp', 0, 0, tiled=False)]
    all_to_all x1, blocking collectives: 45.1 us -> 39.6 us  [per_device(): gathered = lax.all_to_all(spread, 'mp', 0, 0, tiled=False)]
    broadcast_in_dim x0 -> x1, local copies, waits for them, and re-layouts: none -> 2.08 us  [per_device(): spread_w = jnp.broadcast_to(both[None], (holders,) + both.shape)]
  transfers between devices with their start and end apart: 2 -> 2, of which waited for: 2 -> 1; matrix products, arithmetic and copies ran while one was open for 6% -> 3% of each run, Pallas kernels for 0% -> 0%
where the time goes in v2:
time: 155 us
  waiting for transfers between devices  71.3 us (46%)
  blocking collectives  39.6 us (26%)
  starting transfers between devices  14 us (9%)
  between operations  13.5 us (9%)
  matrix products  10.5 us (7%)
  local copies, waits for them, and re-layouts  4.07 us (3%)
  other arithmetic  1.81 us (1%)
    all_to_all x1, waiting for transfers between devices, per_device(): stack = lax.all_to_all(spread_w, 'dp', 0, 0, tiled=False)  70.6 us
    all_to_all x1, blocking collectives, per_device(): gathered = lax.all_to_all(spread, 'mp', 0, 0, tiled=False)  39.6 us
    all_to_all x1, starting transfers between devices, per_device(): stack = lax.all_to_all(spread_w, 'dp', 0, 0, tiled=False)  14 us
    dot_general x1, matrix products, per_device(): jnp.dot(hidden_rows, base_weight, preferred_element_type=jnp.float32)  6.46 us
  transfers between devices with their start and end apart: 2, of which 1 were waited for; matrix products, arithmetic and copies ran while one was open for 3% of the time, Pallas kernels for 0%

profile of v2, /device:TPU:1, one launch (start us, length us, event | category | flops | bytes accessed | tf_op | source)
XLA Modules:
  0.0 154.8 jit_solution(665057527968099825)
XLA Ops:
  6.5 0.0 copy-start
  6.5 0.9 pad_maximum_fusion
  7.5 0.2 copy-done
  7.6 6.5 %convolution_convert_fusion = bf16[512,4096]{1,0:T(8,128)(2,1)} fusion(bf16[512,512]{1,0:T(8,128)(2,1)S(1)} %copy-done, bf16[512,4096]{1,0:T(8,128)(2,1)} %param.7), kind=kOutput, calls=%fused_computation | convolution fusion | flops 2149580800 | bytes 8912896 | tf_op jit(solution)/shard_map/dot_general | solution.py:20
  14.1 2.1 %broadcast_in_dim.64 = bf16[32,64,768]{2,1,0:T(8,128)(2,1)} broadcast(bf16[64,768]{1,0:T(8,128)(2,1)S(1)} %pad_maximum_fusion), dimensions={1,2} | broadcast | bytes 3244032 | tf_op jit(solution)/shard_map/broadcast_in_dim | solution.py:28
  16.2 0.0 copy-start.1
  16.2 0.0 copy-start.2
  16.2 14.0 %all-to-all-start = ((bf16[32,64,768]{2,1,0:T(8,128)(2,1)}), bf16[32,64,768]{2,1,0:T(8,128)(2,1)}, u32[]{:S(2)}, u32[]{:S(2)}) async-start(bf16[32,64,768]{2,1,0:T(8,128)(2,1)} %broadcast_in_dim.64), calls=%async_computation.1 | async-start | bytes 6291456 | tf_op jit(solution)/shard_map/all_to_all | solution.py:29
  30.1 0.0 reduce-scatter.2.cloned.1.call-start
  30.2 0.7 reduce-scatter.2.cloned.1.call-update
  30.9 0.0 copy-done.1
  30.9 0.0 copy-done.2
  30.9 0.1 select_reduce_fusion.1
  31.0 70.6 %all-to-all-done = bf16[32,64,768]{2,1,0:T(8,128)(2,1)} async-done(((bf16[32,64,768]{2,1,0:T(8,128)(2,1)}), bf16[32,64,768]{2,1,0:T(8,128)(2,1)}, u32[]{:S(2)}, u32[]{:S(2)}) %all-to-all-start) | async-done | bytes 3145760 | tf_op jit(solution)/shard_map/all_to_all | solution.py:29
  101.6 1.7 %slice.8 = bf16[32,64,512]{2,1,0:T(8,128)(2,1)S(1)} slice(bf16[32,64,768]{2,1,0:T(8,128)(2,1)} %all-to-all-done), slice={[0:32], [0:64], [0:512]} | slice | bytes 4194304 | tf_op jit(solution)/shard_map/slice | solution.py:30
  103.4 1.3 fusion.22
  104.7 0.6 select_reduce_fusion
  105.3 0.1 broadcast_in_dim.66
  105.4 39.6 %all_to_all.10 = bf16[16,512,64]{1,2,0:T(8,128)(2,1)S(1)} all-to-all(bf16[16,512,64]{1,2,0:T(8,128)(2,1)S(1)} %broadcast_in_dim.66), channel_id=1, replica_groups=mesh['dp'=32,'mp'=16] {'mp'}, dimensions={0} | all-to-all | bytes 2097152 | tf_op jit(solution)/shard_map/all_to_all | solution.py:40
  145.0 0.1 reduce_sum.32
  145.1 0.0 reduce-scatter.2.cloned.1.call-done
  145.2 2.8 %fusion.15 = bf16[512,256]{1,0:T(8,128)(2,1)} fusion(pred[512,32]{0,1:T(8,128)(4,1)S(1)} %iota_compare_fusion, bf16[32,64,768]{2,1,0:T(8,128)(2,1)} %all-to-all-done, bf16[512,64]{0,1:T(8,128)(2,1)S(1)} %reduce_sum.32, bf16[512,256]{1,0:T(8,128)(2,1)} %reduce-scatter.2.cloned.1.call-done), kind=kOutput, calls=%fused_computation.9 | convolution fusion | flops 538574848 | bytes 1654784 | tf_op jit(solution)/shard_map/dot_general | solution.py:44
  (1 shorter events, 0.0 us)
Async XLA Ops:
  6.5 1.1 copy-start
  16.2 14.7 %copy-start.1 = (s32[512,1]{0,1:T(1,128)S(1)}, s32[512,1]{0,1:T(1,128)}, u32[]{:S(2)}) copy-start(s32[512,1]{0,1:T(1,128)} %param.10) | copy-start | bytes 6148
  16.2 14.7 %copy-start.2 = (s32[32]{0:T(128)S(1)}, s32[32]{0:T(128)}, u32[]{:S(2)}) copy-start(s32[32]{0:T(128)} %param.11) | copy-start | bytes 388
  16.2 85.5 %all-to-all-start = ((bf16[32,64,768]{2,1,0:T(8,128)(2,1)}), bf16[32,64,768]{2,1,0:T(8,128)(2,1)}, u32[]{:S(2)}, u32[]{:S(2)}) async-start(bf16[32,64,768]{2,1,0:T(8,128)(2,1)} %broadcast_in_dim.64), calls=%async_computation.1 | async-start | bytes 6291456 | tf_op jit(solution)/shard_map/all_to_all | solution.py:29
  30.1 115.0 %reduce-scatter.2.cloned.1.call-start = ((), (), s32[]{:S(2)}) async-start(), calls=%async_computation.3 | async-start | bytes 4456448 | tf_op jit(solution)/shard_map/reduce_scatter | solution.py:22
Sparse Core Ops, SparseCore 0:
  33.8 66.6 reduce-scatter.1

commit v3 on v2

v3 whole, which is shorter than its diff:
```python
import jax
import jax.numpy as jnp
import numpy as np
from jax import lax
from jax.sharding import Mesh, PartitionSpec as P


def spread_over(block, axis):
    n = lax.axis_size(axis)
    return lax.all_to_all(jnp.broadcast_to(block[None], (n,) + block.shape), axis, 0, 0, tiled=False)


def split_axis(mesh, name):
    lead = [slice(None) if a == name else 0 for a in mesh.axis_names]
    line = mesh.devices[tuple(lead)].reshape(-1)
    parts = []
    for c in range(3):
        n = len({d.coords[c] for d in line})
        if n > 1:
            parts.append((c, n))
    if len({d.core_on_chip for d in line}) > 1:
        parts.append((3, 2))
    return parts


def per_device(hidden_rows, base_weight, adapter_down, adapter_up, adapter_of_row, holder_map):
    row_count, feat_width = hidden_rows.shape
    holders = lax.axis_size(DP)
    n_mp = lax.axis_size(MP)
    rank = adapter_down.shape[1]
    out_width = adapter_up.shape[2]
    adapters = holder_map.shape[0]

    adapter_ids = adapter_of_row[:, 0]
    matches = adapter_ids[:, None] == jnp.arange(adapters, dtype=jnp.int32)[None, :]
    slot_of_row = jnp.sum(jnp.where(matches, holder_map[None, :], 0), axis=1)
    slot_hot = slot_of_row[:, None] == jnp.arange(holders, dtype=jnp.int32)[None, :]

    base_terms = jnp.dot(hidden_rows, base_weight, preferred_element_type=jnp.float32)
    base_bf = base_terms.astype(jnp.bfloat16)
    base_total = lax.psum_scatter(base_bf, MP, scatter_dimension=1, tiled=True).astype(
        jnp.float32
    )

    both = jnp.concatenate([adapter_down[0], adapter_up[0]], axis=1)[None]
    for axis in reversed(DP):
        both = spread_over(both, axis)
    stack = both.reshape(holders, rank, both.shape[-1])
    down_w = stack[:, :, :feat_width]
    up_w = stack[:, :, feat_width:]

    every = jnp.dot(
        hidden_rows,
        down_w.transpose(2, 0, 1).reshape(feat_width, holders * rank),
        preferred_element_type=jnp.float32,
    ).reshape(row_count, holders, rank)
    partial_down = jnp.sum(jnp.where(slot_hot[:, :, None], every, 0.0), axis=1)
    gathered = partial_down.astype(jnp.bfloat16)[None]
    for axis in MP:
        gathered = spread_over(gathered, axis)
    gathered = gathered.reshape(n_mp, row_count, rank)
    down = jnp.sum(gathered.astype(jnp.float32), axis=0).astype(jnp.bfloat16)

    placed = jnp.where(slot_hot[:, :, None], down[:, None, :], jnp.zeros((), jnp.bfloat16))
    lift = jnp.dot(
        placed.reshape(row_count, holders * rank),
        up_w.reshape(holders * rank, out_width),
        preferred_element_type=jnp.float32,
    ).astype(jnp.bfloat16)
    return (base_total + lift.astype(jnp.float32)).astype(jnp.bfloat16)


def coordinate(device, c):
    return device.core_on_chip if c == 3 else device.coords[c]


def fine_mesh(mesh):
    parts = [split_axis(mesh, name) for name in mesh.axis_names]
    names = [tuple(f"{name}{c}" for c, _ in p) for name, p in zip(mesh.axis_names, parts)]
    flat = [q for p in parts for q in p]
    devices = mesh.devices.reshape([n for _, n in flat])
    for k, (c, n) in enumerate(flat):
        for index in np.ndindex(devices.shape):
            if index[k] + 1 < n:
                step = list(index)
                step[k] += 1
                a, b = devices[index], devices[tuple(step)]
                if any((coordinate(a, o) != coordinate(b, o)) != (o == c) for o in range(4)):
                    return mesh, tuple((name,) for name in mesh.axis_names)
    return Mesh(devices, tuple(q for p in names for q in p)), tuple(names)


def solution(mesh):
    global DP, MP
    fine, (DP, MP) = fine_mesh(mesh)
    placed = (
        P(DP, MP),
        P(MP, None),
        P(DP, None, MP),
        P(DP, None, MP),
        P(DP, None),
        P(),
    )
    return jax.shard_map(per_device, mesh=fine, in_specs=placed, out_specs=P(DP, MP), check_vma=False)
```

time: 155 us -> 132 us (0.85)
  waiting for transfers between devices: 71.3 us -> 35.1 us
  blocking collectives: 39.6 us -> 61.5 us
  starting transfers between devices: 14 us -> 4.64 us
  local copies, waits for them, and re-layouts: 4.07 us -> 5.87 us
    all_to_all x1, waiting for transfers between devices: 70.6 us -> 35.1 us  [spread_over(): lax.all_to_all(jnp.broadcast_to(block[None], (n,) + block.shape), axis, 0...]
    all_to_all x1 -> x3, blocking collectives: 39.6 us -> 61.5 us  [spread_over(): lax.all_to_all(jnp.broadcast_to(block[None], (n,) + block.shape), axis, 0...]
    all_to_all x1, starting transfers between devices: 14 us -> 4.64 us  [spread_over(): lax.all_to_all(jnp.broadcast_to(block[None], (n,) + block.shape), axis, 0...]
    unnamed x6 -> x10, local copies, waits for them, and re-layouts: 0.17 us -> 1.86 us
  transfers between devices with their start and end apart: 2 -> 2, of which waited for: 1 -> 1; matrix products, arithmetic and copies ran while one was open for 3% -> 5% of each run, Pallas kernels for 0% -> 0%
where the time goes in v3:
time: 132 us
  blocking collectives  61.5 us (47%)
  waiting for transfers between devices  35.1 us (27%)
  between operations  13.5 us (10%)
  matrix products  10.5 us (8%)
  local copies, waits for them, and re-layouts  5.87 us (4%)
  starting transfers between devices  4.64 us (4%)
    all_to_all x3, blocking collectives, spread_over(): lax.all_to_all(jnp.broadcast_to(block[None], (n,) + block.shape), axis, 0...  61.5 us
    all_to_all x1, waiting for transfers between devices, spread_over(): lax.all_to_all(jnp.broadcast_to(block[None], (n,) + block.shape), axis, 0...  35.1 us
    dot_general x1, matrix products, per_device(): jnp.dot(hidden_rows, base_weight, preferred_element_type=jnp.float32)  6.46 us
    all_to_all x1, starting transfers between devices, spread_over(): lax.all_to_all(jnp.broadcast_to(block[None], (n,) + block.shape), axis, 0...  4.64 us
    dot_general x1, matrix products, per_device(): jnp.dot(placed.reshape(row_count, holders * rank), up_w.reshape(holders *...  2.75 us
  transfers between devices with their start and end apart: 2, of which 1 were waited for; matrix products, arithmetic and copies ran while one was open for 5% of the time, Pallas kernels for 0%

profile of v3, /device:TPU:1, one launch (start us, length us, event | category | flops | bytes accessed | tf_op | source)
XLA Modules:
  0.0 132.0 jit_solution(7535650916951797570)
XLA Ops:
  6.5 0.0 copy-start
  6.5 0.0 reduce-scatter.2.cloned.1.call-start
  6.5 1.0 copy-done
  7.6 6.5 %convolution_convert_fusion = bf16[512,4096]{1,0:T(8,128)(2,1)} fusion(bf16[512,512]{1,0:T(8,128)(2,1)S(1)} %copy-done, bf16[512,4096]{1,0:T(8,128)(2,1)} %param.7), kind=kOutput, calls=%fused_computation | convolution fusion | flops 2149580800 | bytes 8912896 | tf_op jit(solution)/shard_map/dot_general | solution.py:39
  14.0 0.0 copy-start.1
  14.0 0.0 copy-start.2
  14.0 0.0 reduce-scatter.2.cloned.1.call-update
  14.1 0.8 copy-done.1
  14.9 0.0 copy-done.2
  14.9 0.1 broadcast_in_dim.78
  15.0 32.3 %all_to_all.20 = bf16[8,1,64,768]{3,2,1,0:T(8,128)(2,1)S(1)} all-to-all(bf16[8,1,64,768]{3,2,1,0:T(8,128)(2,1)S(1)} %broadcast_in_dim.78), channel_id=1, replica_groups=mesh['dp0'=4,'dp2'=8,'mp1'=8,'mp3'=2] {'dp2'}, dimensions={0} | all-to-all | bytes 1572864 | tf_op jit(solution)/shard_map/all_to_all | solution.py:10
  47.2 0.0 copy-start.3
  47.2 0.0 copy-start.4
  47.2 2.1 %broadcast_in_dim.80 = bf16[4,8,1,64,768]{4,3,1,2,0:T(8,128)(2,1)} broadcast(bf16[8,64,768]{2,1,0:T(8,128)(2,1)S(1)} %bitcast.28), dimensions={1,3,4} | broadcast | bytes 3932160 | tf_op jit(solution)/shard_map/broadcast_in_dim | solution.py:10
  49.3 4.6 %all-to-all-start.1 = ((bf16[4,8,1,64,768]{4,3,1,2,0:T(8,128)(2,1)}), bf16[4,8,1,64,768]{4,3,1,2,0:T(8,128)(2,1)}, u32[]{:S(2)}, u32[]{:S(2)}) async-start(bf16[4,8,1,64,768]{4,3,1,2,0:T(8,128)(2,1)} %broadcast_in_dim.80), calls=%async_computation.2 | async-start | bytes 6291456 | tf_op jit(solution)/shard_map/all_to_all | solution.py:10
  54.0 0.0 copy-done.3
  54.0 0.0 copy-done.4
  54.0 0.1 select_reduce_fusion.1
  54.1 35.1 %all-to-all-done.1 = bf16[4,8,1,64,768]{4,3,1,2,0:T(8,128)(2,1)} async-done(((bf16[4,8,1,64,768]{4,3,1,2,0:T(8,128)(2,1)}), bf16[4,8,1,64,768]{4,3,1,2,0:T(8,128)(2,1)}, u32[]{:S(2)}, u32[]{:S(2)}) %all-to-all-start.1) | async-done | bytes 3145760 | tf_op jit(solution)/shard_map/all_to_all | solution.py:10
  89.2 1.7 %slice.8 = bf16[32,64,512]{2,1,0:T(8,128)(2,1)S(1)} slice(bf16[32,64,768]{2,1,0:T(8,128)(2,1)} %bitcast.4), slice={[0:32], [0:64], [0:512]} | slice | bytes 4194304 | tf_op jit(solution)/shard_map/slice | solution.py:49
  90.9 1.3 fusion.22
  92.2 0.6 select_reduce_fusion
  92.9 19.6 %all_to_all.21 = bf16[8,1,512,64]{2,3,1,0:T(8,128)(2,1)S(1)} all-to-all(bf16[8,1,512,64]{2,3,1,0:T(8,128)(2,1)S(1)} %broadcast_in_dim.82), channel_id=1, replica_groups=mesh['dp0'=4,'dp2'=8,'mp1'=8,'mp3'=2] {'mp1'}, dimensions={0} | all-to-all | bytes 1048576 | tf_op jit(solution)/shard_map/all_to_all | solution.py:10
  112.5 0.1 broadcast_in_dim.84
  112.6 9.7 %all_to_all.22 = bf16[2,8,1,512,64]{3,4,2,1,0:T(8,128)(2,1)S(1)} all-to-all(bf16[2,8,1,512,64]{3,4,2,1,0:T(8,128)(2,1)S(1)} %broadcast_in_dim.84), channel_id=1, replica_groups=mesh['dp0'=4,'dp2'=8,'mp1'=8,'mp3'=2] {'mp3'}, dimensions={0} | all-to-all | bytes 2097152 | tf_op jit(solution)/shard_map/all_to_all | solution.py:10
  122.2 0.1 reduce_sum.32
  122.4 0.0 reduce-scatter.2.cloned.1.call-done
  122.4 2.8 %fusion.15 = bf16[512,256]{1,0:T(8,128)(2,1)} fusion(pred[512,32]{0,1:T(8,128)(4,1)S(1)} %iota_compare_fusion, bf16[32,64,768]{2,1,0:T(8,128)(2,1)} %bitcast.4, bf16[512,64]{0,1:T(8,128)(2,1)S(1)} %reduce_sum.32, bf16[512,256]{1,0:T(8,128)(2,1)} %reduce-scatter.2.cloned.1.call-done), kind=kOutput, calls=%fused_computation.9 | convolution fusion | flops 538574848 | bytes 1654784 | tf_op jit(solution)/shard_map/dot_general | solution.py:65
  (3 shorter events, 0.1 us)
Async XLA Ops:
  6.5 1.0 copy-start
  6.5 115.9 %reduce-scatter.2.cloned.1.call-start = ((), (), s32[]{:S(2)}) async-start(), calls=%async_computation.5 | async-start | bytes 4456448 | tf_op jit(solution)/shard_map/reduce_scatter | solution.py:41
  14.0 0.8 copy-start.1
  14.0 0.8 copy-start.2
  47.2 6.7 %copy-start.3 = (s32[512,1]{0,1:T(1,128)S(1)}, s32[512,1]{0,1:T(1,128)}, u32[]{:S(2)}) copy-start(s32[512,1]{0,1:T(1,128)} %param.10) | copy-start | bytes 6148
  47.2 6.8 %copy-start.4 = (s32[32]{0:T(128)S(1)}, s32[32]{0:T(128)}, u32[]{:S(2)}) copy-start(s32[32]{0:T(128)} %param.11) | copy-start | bytes 388
  49.3 39.9 %all-to-all-start.1 = ((bf16[4,8,1,64,768]{4,3,1,2,0:T(8,128)(2,1)}), bf16[4,8,1,64,768]{4,3,1,2,0:T(8,128)(2,1)}, u32[]{:S(2)}, u32[]{:S(2)}) async-start(bf16[4,8,1,64,768]{4,3,1,2,0:T(8,128)(2,1)} %broadcast_in_dim.80), calls=%async_computation.2 | async-start | bytes 6291456 | tf_op jit(solution)/shard_map/all_to_all | solution.py:10
Sparse Core Ops, SparseCore 0:
  14.2 69.8 reduce-scatter.1

commit v4 on v3

--- a/solution.py
+++ b/solution.py
@@ -36,18 +36,24 @@
     slot_of_row = jnp.sum(jnp.where(matches, holder_map[None, :], 0), axis=1)
     slot_hot = slot_of_row[:, None] == jnp.arange(holders, dtype=jnp.int32)[None, :]
 
+    both = jnp.concatenate([adapter_down[0], adapter_up[0]], axis=1)[None]
+    for axis in reversed(DP):
+        if axis == DP[-1] and len(DP) > 1:
+            both = lax.all_gather(both, axis, axis=0, tiled=False)
+            first_stage = both
+        else:
+            both = spread_over(both, axis)
+    stack = both.reshape(holders, rank, both.shape[-1])
+    down_w = stack[:, :, :feat_width]
+    up_w = stack[:, :, feat_width:]
+
     base_terms = jnp.dot(hidden_rows, base_weight, preferred_element_type=jnp.float32)
     base_bf = base_terms.astype(jnp.bfloat16)
+    if len(DP) > 1:
+        base_bf, first_stage = lax.optimization_barrier((base_bf, first_stage))
     base_total = lax.psum_scatter(base_bf, MP, scatter_dimension=1, tiled=True).astype(
         jnp.float32
     )
-
-    both = jnp.concatenate([adapter_down[0], adapter_up[0]], axis=1)[None]
-    for axis in reversed(DP):
-        both = spread_over(both, axis)
-    stack = both.reshape(holders, rank, both.shape[-1])
-    down_w = stack[:, :, :feat_width]
-    up_w = stack[:, :, feat_width:]
 
     every = jnp.dot(
         hidden_rows,

time: 132 us -> 127 us (0.962)
  blocking collectives: 61.5 us -> 58.6 us
  waiting for transfers between devices: 35.1 us -> 32.4 us
    all_to_all x3 -> x2, blocking collectives: 61.5 us -> 30 us  [spread_over(): lax.all_to_all(jnp.broadcast_to(block[None], (n,) + block.shape), axis, 0...]
    all_gather x0 -> x1, blocking collectives: none -> 28.5 us  [per_device(): both = lax.all_gather(both, axis, axis=0, tiled=False)]
    all_to_all x1, waiting for transfers between devices: 35.1 us -> 32.3 us  [spread_over(): lax.all_to_all(jnp.broadcast_to(block[None], (n,) + block.shape), axis, 0...]
where the time goes in v4:
time: 127 us; the launch traced here: 126 us
  blocking collectives  58.6 us (46%)
  waiting for transfers between devices  32.4 us (26%)
  between operations  13.5 us (11%)
  matrix products  10.5 us (8%)
  local copies, waits for them, and re-layouts  5.86 us (5%)
  starting transfers between devices  4.65 us (4%)
    all_to_all x1, waiting for transfers between devices, spread_over(): lax.all_to_all(jnp.broadcast_to(block[None], (n,) + block.shape), axis, 0...  32.3 us
    all_to_all x2, blocking collectives, spread_over(): lax.all_to_all(jnp.broadcast_to(block[None], (n,) + block.shape), axis, 0...  30 us
    all_gather x1, blocking collectives, per_device(): both = lax.all_gather(both, axis, axis=0, tiled=False)  28.5 us
    dot_general x1, matrix products, per_device(): jnp.dot(hidden_rows, base_weight, preferred_element_type=jnp.float32)  6.46 us
    all_to_all x1, starting transfers between devices, spread_over(): lax.all_to_all(jnp.broadcast_to(block[None], (n,) + block.shape), axis, 0...  4.64 us
    dot_general x1, matrix products, per_device(): jnp.dot(placed.reshape(row_count, holders * rank), up_w.reshape(holders *...  2.75 us
  transfers between devices with their start and end apart: 2, of which 1 were waited for; matrix products, arithmetic and copies ran while one was open for 5% of the time, Pallas kernels for 0%

profile of v4, /device:TPU:1, one launch (start us, length us, event | category | flops | bytes accessed | tf_op | source)
XLA Modules:
  0.0 126.3 jit_solution(7420670950360117546)
XLA Ops:
  6.5 0.0 copy-start
  6.5 0.0 reduce-scatter.2.cloned.1.call-start
  6.5 1.0 copy-done
  7.6 6.5 %convolution_convert_fusion = bf16[512,4096]{1,0:T(8,128)(2,1)} fusion(bf16[512,512]{1,0:T(8,128)(2,1)S(1)} %copy-done, bf16[512,4096]{1,0:T(8,128)(2,1)} %param.7), kind=kOutput, calls=%fused_computation | convolution fusion | flops 2149580800 | bytes 8912896 | tf_op jit(solution)/shard_map/dot_general | solution.py:50
  14.0 0.0 copy-start.1
  14.0 0.0 copy-start.2
  14.0 0.0 reduce-scatter.2.cloned.1.call-update
  14.1 0.8 copy-done.1
  14.9 0.0 copy-done.2
  14.9 28.5 %all-gather = bf16[512,768]{1,0:T(8,128)(2,1)S(1)} all-gather(bf16[64,768]{1,0:T(8,128)(2,1)S(1)} %pad_maximum_fusion), channel_id=2, replica_groups=mesh['dp0'=4,'dp2'=8,'mp1'=8,'mp3'=2] {'dp2'}, dimensions={0}, use_global_device_ids=true | all-gather | bytes 884736 | tf_op jit(solution)/shard_map/all_gather | solution.py:42
  43.4 0.0 copy-start.3
  43.4 0.0 copy-start.4
  43.4 2.1 %broadcast_in_dim.74 = bf16[4,8,1,64,768]{4,3,1,2,0:T(8,128)(2,1)} broadcast(bf16[8,64,768]{2,1,0:T(8,128)(2,1)S(1)} %bitcast.28), dimensions={1,3,4} | broadcast | bytes 3932160 | tf_op jit(solution)/shard_map/broadcast_in_dim | solution.py:10
  45.5 4.6 %all-to-all-start = ((bf16[4,8,1,64,768]{4,3,1,2,0:T(8,128)(2,1)}), bf16[4,8,1,64,768]{4,3,1,2,0:T(8,128)(2,1)}, u32[]{:S(2)}, u32[]{:S(2)}) async-start(bf16[4,8,1,64,768]{4,3,1,2,0:T(8,128)(2,1)} %broadcast_in_dim.74), calls=%async_computation.1 | async-start | bytes 6291456 | tf_op jit(solution)/shard_map/all_to_all | solution.py:10
  50.2 0.0 copy-done.3
  50.2 0.0 copy-done.4
  50.2 0.1 select_reduce_fusion.1
  50.3 32.3 %all-to-all-done = bf16[4,8,1,64,768]{4,3,1,2,0:T(8,128)(2,1)} async-done(((bf16[4,8,1,64,768]{4,3,1,2,0:T(8,128)(2,1)}), bf16[4,8,1,64,768]{4,3,1,2,0:T(8,128)(2,1)}, u32[]{:S(2)}, u32[]{:S(2)}) %all-to-all-start) | async-done | bytes 3145760 | tf_op jit(solution)/shard_map/all_to_all | solution.py:10
  82.7 1.8 %slice.8 = bf16[32,64,512]{2,1,0:T(8,128)(2,1)S(1)} slice(bf16[32,64,768]{2,1,0:T(8,128)(2,1)} %bitcast.4), slice={[0:32], [0:64], [0:512]} | slice | bytes 4194304 | tf_op jit(solution)/shard_map/slice | solution.py:47
  84.4 1.3 %fusion.22 = f32[2048,512]{1,0:T(8,128)S(1)} fusion(bf16[512,2048]{0,1:T(8,128)(2,1)S(1)} %bitcast.27, bf16[512,512]{1,0:T(8,128)(2,1)S(1)} %copy-done), kind=kOutput, calls=%fused_computation.18 | convolution fusion | flops 1073741824 | bytes 6815744 | tf_op jit(solution)/shard_map/dot_general | solution.py:58
  85.7 0.6 select_reduce_fusion
  86.4 17.6 %all_to_all.15 = bf16[8,1,512,64]{2,3,1,0:T(8,128)(2,1)S(1)} all-to-all(bf16[8,1,512,64]{2,3,1,0:T(8,128)(2,1)S(1)} %broadcast_in_dim.76), channel_id=1, replica_groups=mesh['dp0'=4,'dp2'=8,'mp1'=8,'mp3'=2] {'mp1'}, dimensions={0} | all-to-all | bytes 1048576 | tf_op jit(solution)/shard_map/all_to_all | solution.py:10
  104.0 0.1 broadcast_in_dim.78
  104.1 12.4 %all_to_all.16 = bf16[2,8,1,512,64]{3,4,2,1,0:T(8,128)(2,1)S(1)} all-to-all(bf16[2,8,1,512,64]{3,4,2,1,0:T(8,128)(2,1)S(1)} %broadcast_in_dim.78), channel_id=1, replica_groups=mesh['dp0'=4,'dp2'=8,'mp1'=8,'mp3'=2] {'mp3'}, dimensions={0} | all-to-all | bytes 2097152 | tf_op jit(solution)/shard_map/all_to_all | solution.py:10
  116.5 0.1 reduce_sum.32
  116.7 0.0 reduce-scatter.2.cloned.1.call-done
  116.7 2.8 %fusion.15 = bf16[512,256]{1,0:T(8,128)(2,1)} fusion(pred[512,32]{0,1:T(8,128)(4,1)S(1)} %iota_compare_fusion, bf16[32,64,768]{2,1,0:T(8,128)(2,1)} %bitcast.4, bf16[512,64]{0,1:T(8,128)(2,1)S(1)} %reduce_sum.32, bf16[512,256]{1,0:T(8,128)(2,1)} %reduce-scatter.2.cloned.1.call-done), kind=kOutput, calls=%fused_computation.9 | convolution fusion | flops 538574848 | bytes 1654784 | tf_op jit(solution)/shard_map/dot_general | solution.py:71
  (3 shorter events, 0.1 us)
Async XLA Ops:
  6.5 1.0 copy-start
  6.5 110.2 %reduce-scatter.2.cloned.1.call-start = ((), (), s32[]{:S(2)}) async-start(), calls=%async_computation.4 | async-start | bytes 4456448 | tf_op jit(solution)/shard_map/reduce_scatter | solution.py:54
  14.0 0.8 copy-start.1
  14.0 0.8 copy-start.2
  43.4 6.7 %copy-start.3 = (s32[512,1]{0,1:T(1,128)S(1)}, s32[512,1]{0,1:T(1,128)}, u32[]{:S(2)}) copy-start(s32[512,1]{0,1:T(1,128)} %param.10) | copy-start | bytes 6148
  43.4 6.8 %copy-start.4 = (s32[32]{0:T(128)S(1)}, s32[32]{0:T(128)}, u32[]{:S(2)}) copy-start(s32[32]{0:T(128)} %param.11) | copy-start | bytes 388
  45.5 37.1 %all-to-all-start = ((bf16[4,8,1,64,768]{4,3,1,2,0:T(8,128)(2,1)}), bf16[4,8,1,64,768]{4,3,1,2,0:T(8,128)(2,1)}, u32[]{:S(2)}, u32[]{:S(2)}) async-start(bf16[4,8,1,64,768]{4,3,1,2,0:T(8,128)(2,1)} %broadcast_in_dim.74), calls=%async_computation.1 | async-start | bytes 6291456 | tf_op jit(solution)/shard_map/all_to_all | solution.py:10
Sparse Core Ops, SparseCore 0:
  14.2 69.6 reduce-scatter.1

commit v5 on v4

--- a/solution.py
+++ b/solution.py
@@ -63,7 +63,10 @@
     partial_down = jnp.sum(jnp.where(slot_hot[:, :, None], every, 0.0), axis=1)
     gathered = partial_down.astype(jnp.bfloat16)[None]
     for axis in MP:
-        gathered = spread_over(gathered, axis)
+        if axis == MP[0] and len(MP) > 1:
+            gathered = lax.all_gather(gathered, axis, axis=0, tiled=False)
+        else:
+            gathered = spread_over(gathered, axis)
     gathered = gathered.reshape(n_mp, row_count, rank)
     down = jnp.sum(gathered.astype(jnp.float32), axis=0).astype(jnp.bfloat16)
 

time: 127 us -> 134 us (1.055)
  blocking collectives: 58.6 us -> 65.5 us
    all_gather x0 -> x1, blocking collectives: none -> 19.4 us  [per_device(): gathered = lax.all_gather(gathered, axis, axis=0, tiled=False)]
    all_to_all x2 -> x1, blocking collectives: 30 us -> 17.6 us  [spread_over(): lax.all_to_all(jnp.broadcast_to(block[None], (n,) + block.shape), axis, 0...]
where the time goes in v5:
time: 134 us; the launch traced here: 133 us
  blocking collectives  65.5 us (49%)
  waiting for transfers between devices  32.4 us (24%)
  between operations  13.5 us (10%)
  matrix products  10.5 us (8%)
  local copies, waits for them, and re-layouts  5.86 us (4%)
  starting transfers between devices  4.65 us (3%)
    all_to_all x1, waiting for transfers between devices, spread_over(): lax.all_to_all(jnp.broadcast_to(block[None], (n,) + block.shape), axis, 0...  32.3 us
    all_gather x1, blocking collectives, per_device(): both = lax.all_gather(both, axis, axis=0, tiled=False)  28.5 us
    all_gather x1, blocking collectives, per_device(): gathered = lax.all_gather(gathered, axis, axis=0, tiled=False)  19.4 us
    all_to_all x1, blocking collectives, spread_over(): lax.all_to_all(jnp.broadcast_to(block[None], (n,) + block.shape), axis, 0...  17.6 us
    dot_general x1, matrix products, per_device(): jnp.dot(hidden_rows, base_weight, preferred_element_type=jnp.float32)  6.46 us
    all_to_all x1, starting transfers between devices, spread_over(): lax.all_to_all(jnp.broadcast_to(block[None], (n,) + block.shape), axis, 0...  4.64 us
    dot_general x1, matrix products, per_device(): jnp.dot(placed.reshape(row_count, holders * rank), up_w.reshape(holders *...  2.76 us
  transfers between devices with their start and end apart: 2, of which 1 were waited for; matrix products, arithmetic and copies ran while one was open for 5% of the time, Pallas kernels for 0%

profile of v5, /device:TPU:1, one launch (start us, length us, event | category | flops | bytes accessed | tf_op | source)
XLA Modules:
  0.0 133.2 jit_solution(13858923890109509115)
XLA Ops:
  6.5 0.0 copy-start
  6.5 0.0 reduce-scatter.2.cloned.1.call-start
  6.5 1.0 copy-done
  7.6 6.5 %convolution_convert_fusion = bf16[512,4096]{1,0:T(8,128)(2,1)} fusion(bf16[512,512]{1,0:T(8,128)(2,1)S(1)} %copy-done, bf16[512,4096]{1,0:T(8,128)(2,1)} %param.7), kind=kOutput, calls=%fused_computation | convolution fusion | flops 2149580800 | bytes 8912896 | tf_op jit(solution)/shard_map/dot_general | solution.py:50
  14.0 0.0 copy-start.1
  14.0 0.0 copy-start.2
  14.0 0.0 reduce-scatter.2.cloned.1.call-update
  14.1 0.8 copy-done.1
  14.9 0.0 copy-done.2
  14.9 28.5 %all-gather = bf16[512,768]{1,0:T(8,128)(2,1)S(1)} all-gather(bf16[64,768]{1,0:T(8,128)(2,1)S(1)} %pad_maximum_fusion), channel_id=2, replica_groups=mesh['dp0'=4,'dp2'=8,'mp1'=8,'mp3'=2] {'dp2'}, dimensions={0}, use_global_device_ids=true | all-gather | bytes 884736 | tf_op jit(solution)/shard_map/all_gather | solution.py:42
  43.4 0.0 copy-start.3
  43.4 0.0 copy-start.4
  43.4 2.1 %broadcast_in_dim.69 = bf16[4,8,1,64,768]{4,3,1,2,0:T(8,128)(2,1)} broadcast(bf16[8,64,768]{2,1,0:T(8,128)(2,1)S(1)} %bitcast.31), dimensions={1,3,4} | broadcast | bytes 3932160 | tf_op jit(solution)/shard_map/broadcast_in_dim | solution.py:10
  45.5 4.6 %all-to-all-start = ((bf16[4,8,1,64,768]{4,3,1,2,0:T(8,128)(2,1)}), bf16[4,8,1,64,768]{4,3,1,2,0:T(8,128)(2,1)}, u32[]{:S(2)}, u32[]{:S(2)}) async-start(bf16[4,8,1,64,768]{4,3,1,2,0:T(8,128)(2,1)} %broadcast_in_dim.69), calls=%async_computation.1 | async-start | bytes 6291456 | tf_op jit(solution)/shard_map/all_to_all | solution.py:10
  50.2 0.0 copy-done.3
  50.2 0.0 copy-done.4
  50.2 0.1 select_reduce_fusion.1
  50.3 32.3 %all-to-all-done = bf16[4,8,1,64,768]{4,3,1,2,0:T(8,128)(2,1)} async-done(((bf16[4,8,1,64,768]{4,3,1,2,0:T(8,128)(2,1)}), bf16[4,8,1,64,768]{4,3,1,2,0:T(8,128)(2,1)}, u32[]{:S(2)}, u32[]{:S(2)}) %all-to-all-start) | async-done | bytes 3145760 | tf_op jit(solution)/shard_map/all_to_all | solution.py:10
  82.7 1.8 %slice.8 = bf16[32,64,512]{2,1,0:T(8,128)(2,1)S(1)} slice(bf16[32,64,768]{2,1,0:T(8,128)(2,1)} %bitcast.4), slice={[0:32], [0:64], [0:512]} | slice | bytes 4194304 | tf_op jit(solution)/shard_map/slice | solution.py:47
  84.4 1.3 fusion.22
  85.7 0.6 select_reduce_fusion
  86.4 19.4 %all-gather.1 = bf16[4096,64]{0,1:T(8,128)(2,1)S(1)} all-gather(bf16[512,64]{0,1:T(8,128)(2,1)S(1)} %select_reduce_fusion), channel_id=3, replica_groups=mesh['dp0'=4,'dp2'=8,'mp1'=8,'mp3'=2] {'mp1'}, dimensions={0}, use_global_device_ids=true | all-gather | bytes 589824 | tf_op jit(solution)/shard_map/all_gather | solution.py:67
  105.8 0.1 broadcast_in_dim.72
  105.9 17.6 %all_to_all.10 = bf16[2,8,1,512,64]{3,4,2,1,0:T(8,128)(2,1)S(1)} all-to-all(bf16[2,8,1,512,64]{3,4,2,1,0:T(8,128)(2,1)S(1)} %broadcast_in_dim.72), channel_id=1, replica_groups=mesh['dp0'=4,'dp2'=8,'mp1'=8,'mp3'=2] {'mp3'}, dimensions={0} | all-to-all | bytes 2097152 | tf_op jit(solution)/shard_map/all_to_all | solution.py:10
  123.5 0.1 reduce_sum.32
  123.6 0.0 reduce-scatter.2.cloned.1.call-done
  123.6 2.8 %fusion.15 = bf16[512,256]{1,0:T(8,128)(2,1)} fusion(pred[512,32]{0,1:T(8,128)(4,1)S(1)} %iota_compare_fusion, bf16[32,64,768]{2,1,0:T(8,128)(2,1)} %bitcast.4, bf16[512,64]{0,1:T(8,128)(2,1)S(1)} %reduce_sum.32, bf16[512,256]{1,0:T(8,128)(2,1)} %reduce-scatter.2.cloned.1.call-done), kind=kOutput, calls=%fused_computation.9 | convolution fusion | flops 538574848 | bytes 1654784 | tf_op jit(solution)/shard_map/dot_general | solution.py:74
  (3 shorter events, 0.1 us)
Async XLA Ops:
  6.5 1.0 copy-start
  6.5 117.1 %reduce-scatter.2.cloned.1.call-start = ((), (), s32[]{:S(2)}) async-start(), calls=%async_computation.3 | async-start | bytes 4456448 | tf_op jit(solution)/shard_map/reduce_scatter | solution.py:54
  14.0 0.8 copy-start.1
  14.0 0.8 copy-start.2
  43.4 6.7 %copy-start.3 = (s32[512,1]{0,1:T(1,128)S(1)}, s32[512,1]{0,1:T(1,128)}, u32[]{:S(2)}) copy-start(s32[512,1]{0,1:T(1,128)} %param.10) | copy-start | bytes 6148
  43.4 6.8 %copy-start.4 = (s32[32]{0:T(128)S(1)}, s32[32]{0:T(128)}, u32[]{:S(2)}) copy-start(s32[32]{0:T(128)} %param.11) | copy-start | bytes 388
  45.5 37.1 %all-to-all-start = ((bf16[4,8,1,64,768]{4,3,1,2,0:T(8,128)(2,1)}), bf16[4,8,1,64,768]{4,3,1,2,0:T(8,128)(2,1)}, u32[]{:S(2)}, u32[]{:S(2)}) async-start(bf16[4,8,1,64,768]{4,3,1,2,0:T(8,128)(2,1)} %broadcast_in_dim.69), calls=%async_computation.1 | async-start | bytes 6291456 | tf_op jit(solution)/shard_map/all_to_all | solution.py:10
Sparse Core Ops, SparseCore 0:
  14.2 69.6 reduce-scatter.1

commit v6 on v4

--- a/solution.py
+++ b/solution.py
@@ -51,9 +51,13 @@
     base_bf = base_terms.astype(jnp.bfloat16)
     if len(DP) > 1:
         base_bf, first_stage = lax.optimization_barrier((base_bf, first_stage))
-    base_total = lax.psum_scatter(base_bf, MP, scatter_dimension=1, tiled=True).astype(
-        jnp.float32
-    )
+    total = base_bf.reshape(row_count, *[lax.axis_size(a) for a in MP], -1)
+    for k in reversed(range(len(MP))):
+        total = lax.all_to_all(total, MP[k], 1 + k, 1 + k, tiled=True)
+        total = jnp.sum(total.astype(jnp.float32), axis=1 + k, keepdims=True)
+        if k:
+            total = total.astype(jnp.bfloat16)
+    base_total = total.reshape(row_count, -1)
 
     every = jnp.dot(
         hidden_rows,

time: 127 us -> 172 us (1.35)
  waiting for transfers between devices: 32.4 us -> 71.8 us
  blocking collectives: 58.6 us -> 33.6 us
  starting transfers between devices: 4.65 us -> 27.5 us
  between operations: 13.5 us -> 0.07 us
  local copies, waits for them, and re-layouts: 5.86 us -> 19 us
  other arithmetic: 0.9 us -> 7.74 us
    all_to_all x0 -> x2, waiting for transfers between devices: none -> 47.3 us  [per_device(): total = lax.all_to_all(total, MP[k], 1 + k, 1 + k, tiled=True)]
    all_to_all x2 -> x1, blocking collectives: 30 us -> 5.49 us  [spread_over(): lax.all_to_all(jnp.broadcast_to(block[None], (n,) + block.shape), axis, 0...]
    all_to_all x0 -> x2, starting transfers between devices: none -> 16 us  [per_device(): total = lax.all_to_all(total, MP[k], 1 + k, 1 + k, tiled=True)]
    reshape x0 -> x2, local copies, waits for them, and re-layouts: none -> 12.5 us  [per_device(): total = base_bf.reshape(row_count, *[lax.axis_size(a) for a in MP], -1)]
    all_to_all x1 -> x2, waiting for transfers between devices: 32.3 us -> 24.4 us  [spread_over(): lax.all_to_all(jnp.broadcast_to(block[None], (n,) + block.shape), axis, 0...]
    all_to_all x1 -> x2, starting transfers between devices: 4.64 us -> 11.5 us  [spread_over(): lax.all_to_all(jnp.broadcast_to(block[None], (n,) + block.shape), axis, 0...]
    reduce_sum x0 -> x2, other arithmetic: none -> 4.7 us  [per_device(): total = jnp.sum(total.astype(jnp.float32), axis=1 + k, keepdims=True)]
    unnamed x10 -> x6, local copies, waits for them, and re-layouts: 1.86 us -> 0.01 us
  transfers between devices with their start and end apart: 2 -> 4, of which waited for: 1 -> 4; matrix products, arithmetic and copies ran while one was open for 5% -> 18% of each run, Pallas kernels for 0% -> 0%
where the time goes in v6:
time: 172 us; the launch traced here: 170 us
  waiting for transfers between devices  71.8 us (42%)
  blocking collectives  33.6 us (20%)
  starting transfers between devices  27.5 us (16%)
  local copies, waits for them, and re-layouts  19 us (11%)
  matrix products  10.4 us (6%)
  other arithmetic  7.74 us (4%)
    all_to_all x2, waiting for transfers between devices, per_device(): total = lax.all_to_all(total, MP[k], 1 + k, 1 + k, tiled=True)  47.3 us
    all_gather x1, blocking collectives, per_device(): both = lax.all_gather(both, axis, axis=0, tiled=False)  28.1 us
    all_to_all x2, waiting for transfers between devices, spread_over(): lax.all_to_all(jnp.broadcast_to(block[None], (n,) + block.shape), axis, 0...  24.4 us
    all_to_all x2, starting transfers between devices, per_device(): total = lax.all_to_all(total, MP[k], 1 + k, 1 + k, tiled=True)  16 us
    reshape x2, local copies, waits for them, and re-layouts, per_device(): total = base_bf.reshape(row_count, *[lax.axis_size(a) for a in MP], -1)  12.5 us
    all_to_all x2, starting transfers between devices, spread_over(): lax.all_to_all(jnp.broadcast_to(block[None], (n,) + block.shape), axis, 0...  11.5 us
    dot_general x1, matrix products, per_device(): jnp.dot(hidden_rows, base_weight, preferred_element_type=jnp.float32)  6.47 us
    all_to_all x1, blocking collectives, spread_over(): lax.all_to_all(jnp.broadcast_to(block[None], (n,) + block.shape), axis, 0...  5.49 us
  transfers between devices with their start and end apart: 4, of which 4 were waited for; matrix products, arithmetic and copies ran while one was open for 18% of the time, Pallas kernels for 0%

profile of v6, /device:TPU:1, one launch (start us, length us, event | category | flops | bytes accessed | tf_op | source)
XLA Modules:
  0.0 170.2 jit_solution(8193130040113002385)
XLA Ops:
  0.0 0.0 copy-start
  0.0 0.9 pad_maximum_fusion
  0.9 28.1 %all-gather = bf16[512,768]{1,0:T(8,128)(2,1)S(1)} all-gather(bf16[64,768]{1,0:T(8,128)(2,1)S(1)} %pad_maximum_fusion), channel_id=2, replica_groups=mesh['dp0'=4,'dp2'=8,'mp1'=8,'mp3'=2] {'dp2'}, dimensions={0}, use_global_device_ids=true | all-gather | bytes 884736 | tf_op jit(solution)/shard_map/all_gather | solution.py:42
  29.0 2.1 %broadcast_in_dim.75 = bf16[4,8,1,64,768]{4,3,1,2,0:T(8,128)(2,1)} broadcast(bf16[8,64,768]{2,1,0:T(8,128)(2,1)S(1)} %bitcast.30), dimensions={1,3,4} | broadcast | bytes 3932160 | tf_op jit(solution)/shard_map/broadcast_in_dim | solution.py:10
  31.1 4.7 %all-to-all-start.2 = ((bf16[4,8,1,64,768]{4,3,1,2,0:T(8,128)(2,1)}), bf16[4,8,1,64,768]{4,3,1,2,0:T(8,128)(2,1)}, u32[]{:S(2)}, u32[]{:S(2)}) async-start(bf16[4,8,1,64,768]{4,3,1,2,0:T(8,128)(2,1)} %broadcast_in_dim.75), calls=%async_computation.2 | async-start | bytes 6291456 | tf_op jit(solution)/shard_map/all_to_all | solution.py:10
  35.8 0.0 copy-done
  35.9 6.5 %convolution_convert_fusion = bf16[512,4096]{1,0:T(8,128)(2,1)} fusion(bf16[512,512]{1,0:T(8,128)(2,1)S(1)} %copy-done, bf16[512,4096]{1,0:T(8,128)(2,1)} %param.7), kind=kOutput, calls=%fused_computation | convolution fusion | flops 2149580800 | bytes 8912896 | tf_op jit(solution)/shard_map/dot_general | solution.py:50
  42.3 7.8 %reshape.60 = bf16[512,8,2,256]{3,2,1,0:T(2,128)(2,1)} reshape(bf16[512,4096]{1,0:T(8,128)(2,1)} %convolution_convert_fusion) | data formatting | bytes 8388608 | tf_op jit(solution)/shard_map/reshape | solution.py:54
  50.1 0.0 copy-start.1
  50.1 0.0 copy-start.2
  50.1 4.7 %copy.10 = bf16[512,8,2,256]{3,1,0,2:T(8,128)(2,1)} copy(bf16[512,8,2,256]{3,2,1,0:T(2,128)(2,1)} %reshape.60) | data formatting | bytes 8388608 | tf_op jit(solution)/shard_map/reshape | solution.py:54
  54.8 0.0 copy-done.1
  54.8 0.0 copy-done.2
  54.8 0.1 select_reduce_fusion.1
  54.9 12.7 %all-to-all-done.2 = bf16[4,8,1,64,768]{4,3,1,2,0:T(8,128)(2,1)} async-done(((bf16[4,8,1,64,768]{4,3,1,2,0:T(8,128)(2,1)}), bf16[4,8,1,64,768]{4,3,1,2,0:T(8,128)(2,1)}, u32[]{:S(2)}, u32[]{:S(2)}) %all-to-all-start.2) | async-done | bytes 3145760 | tf_op jit(solution)/shard_map/all_to_all | solution.py:10
  67.6 12.4 %all-to-all-start = ((bf16[512,8,2,256]{3,1,0,2:T(8,128)(2,1)}), bf16[512,8,2,256]{3,1,0,2:T(8,128)(2,1)}, u32[]{:S(2)}, u32[]{:S(2)}) async-start(bf16[512,8,2,256]{3,1,0,2:T(8,128)(2,1)} %copy.10), calls=%async_computation | async-start | bytes 8388608 | tf_op jit(solution)/shard_map/all_to_all | solution.py:56
  80.0 1.7 %slice.8 = bf16[32,64,512]{2,1,0:T(8,128)(2,1)S(1)} slice(bf16[32,64,768]{2,1,0:T(8,128)(2,1)} %bitcast.5), slice={[0:32], [0:64], [0:512]} | slice | bytes 4194304 | tf_op jit(solution)/shard_map/slice | solution.py:47
  81.7 1.3 fusion.22
  83.0 0.6 select_reduce_fusion
  83.7 0.5 all-to-all-done
  84.1 0.8 broadcast_in_dim.77
  85.0 6.8 %all-to-all-start.3 = ((bf16[8,1,512,64]{2,3,1,0:T(8,128)(2,1)}), bf16[8,1,512,64]{2,3,1,0:T(8,128)(2,1)S(1)}, u32[]{:S(2)}, u32[]{:S(2)}) async-start(bf16[8,1,512,64]{2,3,1,0:T(8,128)(2,1)} %broadcast_in_dim.77), calls=%async_computation.3 | async-start | bytes 1048576 | tf_op jit(solution)/shard_map/all_to_all | solution.py:10
  91.8 4.4 %reduce_sum.51 = bf16[512,8,256]{2,1,0:T(8,128)(2,1)S(1)} reduce(bf16[512,8,2,256]{3,1,0,2:T(8,128)(2,1)} %all-to-all-done, bf16[]{:T(256)} %constant.2.clone.1), dimensions={2}, to_apply=%region_0.1 | reduce | flops 1048576 | bytes 6291458 | tf_op jit(solution)/shard_map/reduce_sum | solution.py:57
  96.2 1.8 %copy.11 = bf16[512,8,1,256]{3,0,2,1:T(8,128)(2,1)} copy(bf16[512,8,1,256]{3,1,0,2:T(8,128)(2,1)S(1)} %bitcast.29) | data formatting | bytes 4194304 | tf_op jit(solution)/shard_map/convert_element_type | solution.py:59
  98.0 11.8 %all-to-all-done.3 = bf16[8,1,512,64]{2,3,1,0:T(8,128)(2,1)S(1)} async-done(((bf16[8,1,512,64]{2,3,1,0:T(8,128)(2,1)}), bf16[8,1,512,64]{2,3,1,0:T(8,128)(2,1)S(1)}, u32[]{:S(2)}, u32[]{:S(2)}) %all-to-all-start.3) | async-done | bytes 524320 | tf_op jit(solution)/shard_map/all_to_all | solution.py:10
  109.8 0.1 broadcast_in_dim.79
  109.9 5.5 %all_to_all.25 = bf16[2,8,1,512,64]{3,4,2,1,0:T(8,128)(2,1)} all-to-all(bf16[2,8,1,512,64]{3,4,2,1,0:T(8,128)(2,1)S(1)} %broadcast_in_dim.79), channel_id=1, replica_groups=mesh['dp0'=4,'dp2'=8,'mp1'=8,'mp3'=2] {'mp3'}, dimensions={0} | all-to-all | bytes 2097152 | tf_op jit(solution)/shard_map/all_to_all | solution.py:10
  115.3 3.6 %all-to-all-start.1 = ((bf16[512,8,1,256]{3,0,2,1:T(8,128)(2,1)}), bf16[512,8,1,256]{3,0,2,1:T(8,128)(2,1)S(1)}, u32[]{:S(2)}, u32[]{:S(2)}) async-start(bf16[512,8,1,256]{3,0,2,1:T(8,128)(2,1)} %copy.11), calls=%async_computation.1 | async-start | bytes 4194304 | tf_op jit(solution)/shard_map/all_to_all | solution.py:56
  119.0 1.4 reduce_sum.55
  120.3 46.8 %all-to-all-done.1 = bf16[512,8,1,256]{3,0,2,1:T(8,128)(2,1)S(1)} async-done(((bf16[512,8,1,256]{3,0,2,1:T(8,128)(2,1)}), bf16[512,8,1,256]{3,0,2,1:T(8,128)(2,1)S(1)}, u32[]{:S(2)}, u32[]{:S(2)}) %all-to-all-start.1) | async-done | bytes 2097184 | tf_op jit(solution)/shard_map/all_to_all | solution.py:56
  167.2 0.3 convert_reduce_fusion
  167.5 2.7 %fusion.15 = bf16[512,256]{1,0:T(8,128)(2,1)} fusion(f32[512,256]{1,0:T(8,128)S(1)} %convert_reduce_fusion, pred[512,32]{0,1:T(8,128)(4,1)S(1)} %iota_compare_fusion, bf16[32,64,768]{2,1,0:T(8,128)(2,1)} %bitcast.5, bf16[512,64]{0,1:T(8,128)(2,1)S(1)} %reduce_sum.55), kind=kOutput, calls=%fused_computation.10 | convolution fusion | flops 538443776 | bytes 1916928 | tf_op jit(solution)/shard_map/dot_general | solution.py:75
  (1 shorter events, 0.0 us)
Async XLA Ops:
  0.0 35.8 %copy-start = (bf16[512,512]{1,0:T(8,128)(2,1)S(1)}, bf16[512,512]{1,0:T(8,128)(2,1)}, u32[]{:S(2)}) copy-start(bf16[512,512]{1,0:T(8,128)(2,1)} %param.6) | copy-start | bytes 1572868
  31.1 36.5 %all-to-all-start.2 = ((bf16[4,8,1,64,768]{4,3,1,2,0:T(8,128)(2,1)}), bf16[4,8,1,64,768]{4,3,1,2,0:T(8,128)(2,1)}, u32[]{:S(2)}, u32[]{:S(2)}) async-start(bf16[4,8,1,64,768]{4,3,1,2,0:T(8,128)(2,1)} %broadcast_in_dim.75), calls=%async_computation.2 | async-start | bytes 6291456 | tf_op jit(solution)/shard_map/all_to_all | solution.py:10
  50.1 4.7 %copy-start.1 = (s32[512,1]{0,1:T(1,128)S(1)}, s32[512,1]{0,1:T(1,128)}, u32[]{:S(2)}) copy-start(s32[512,1]{0,1:T(1,128)} %param.10) | copy-start | bytes 6148
  50.1 4.7 %copy-start.2 = (s32[32]{0:T(128)S(1)}, s32[32]{0:T(128)}, u32[]{:S(2)}) copy-start(s32[32]{0:T(128)} %param.11) | copy-start | bytes 388
  67.6 16.5 %all-to-all-start = ((bf16[512,8,2,256]{3,1,0,2:T(8,128)(2,1)}), bf16[512,8,2,256]{3,1,0,2:T(8,128)(2,1)}, u32[]{:S(2)}, u32[]{:S(2)}) async-start(bf16[512,8,2,256]{3,1,0,2:T(8,128)(2,1)} %copy.10), calls=%async_computation | async-start | bytes 8388608 | tf_op jit(solution)/shard_map/all_to_all | solution.py:56
  85.0 24.8 %all-to-all-start.3 = ((bf16[8,1,512,64]{2,3,1,0:T(8,128)(2,1)}), bf16[8,1,512,64]{2,3,1,0:T(8,128)(2,1)S(1)}, u32[]{:S(2)}, u32[]{:S(2)}) async-start(bf16[8,1,512,64]{2,3,1,0:T(8,128)(2,1)} %broadcast_in_dim.77), calls=%async_computation.3 | async-start | bytes 1048576 | tf_op jit(solution)/shard_map/all_to_all | solution.py:10
  115.3 51.8 %all-to-all-start.1 = ((bf16[512,8,1,256]{3,0,2,1:T(8,128)(2,1)}), bf16[512,8,1,256]{3,0,2,1:T(8,128)(2,1)S(1)}, u32[]{:S(2)}, u32[]{:S(2)}) async-start(bf16[512,8,1,256]{3,0,2,1:T(8,128)(2,1)} %copy.11), calls=%async_computation.1 | async-start | bytes 4194304 | tf_op jit(solution)/shard_map/all_to_all | solution.py:56

commit v7 on v3

--- a/solution.py
+++ b/solution.py
@@ -36,18 +36,23 @@
     slot_of_row = jnp.sum(jnp.where(matches, holder_map[None, :], 0), axis=1)
     slot_hot = slot_of_row[:, None] == jnp.arange(holders, dtype=jnp.int32)[None, :]
 
+    both = jnp.concatenate([adapter_down[0], adapter_up[0]], axis=1)[None]
+    both = lax.all_gather(both, DP[-1], axis=0, tiled=False)
+    down_w = both[..., :feat_width]
+    up_w = both[..., feat_width:]
+    for axis in reversed(DP[:-1]):
+        down_w = spread_over(down_w, axis)
+    down_w = down_w.reshape(holders, rank, feat_width)
+
     base_terms = jnp.dot(hidden_rows, base_weight, preferred_element_type=jnp.float32)
     base_bf = base_terms.astype(jnp.bfloat16)
     base_total = lax.psum_scatter(base_bf, MP, scatter_dimension=1, tiled=True).astype(
         jnp.float32
     )
-
-    both = jnp.concatenate([adapter_down[0], adapter_up[0]], axis=1)[None]
-    for axis in reversed(DP):
-        both = spread_over(both, axis)
-    stack = both.reshape(holders, rank, both.shape[-1])
-    down_w = stack[:, :, :feat_width]
-    up_w = stack[:, :, feat_width:]
+    up_w, base_total = lax.optimization_barrier((up_w, base_total))
+    for axis in reversed(DP[:-1]):
+        up_w = lax.all_gather(up_w, axis, axis=0, tiled=False)
+    up_w = up_w.reshape(holders, rank, out_width)
 
     every = jnp.dot(
         hidden_rows,

time: 132 us -> 126 us (0.955)
  blocking collectives: 61.5 us -> 57.4 us
  waiting for transfers between devices: 35.1 us -> 33.2 us
  local copies, waits for them, and re-layouts: 5.87 us -> 4.32 us
    all_to_all x1, waiting for transfers between devices: 35.1 us -> 0.01 us  [spread_over(): lax.all_to_all(jnp.broadcast_to(block[None], (n,) + block.shape), axis, 0...]
    reduce_scatter x1, waiting for transfers between devices: 0.02 us -> 33.1 us  [per_device(): lax.psum_scatter(base_bf, MP, scatter_dimension=1, tiled=True)]
    all_to_all x3 -> x2, blocking collectives: 61.5 us -> 28.8 us  [spread_over(): lax.all_to_all(jnp.broadcast_to(block[None], (n,) + block.shape), axis, 0...]
    all_gather x0 -> x1, blocking collectives: none -> 28.5 us  [per_device(): both = lax.all_gather(both, DP[-1], axis=0, tiled=False)]
  transfers between devices with their start and end apart: 2 -> 3, of which waited for: 1 -> 1; matrix products, arithmetic and copies ran while one was open for 5% -> 5% of each run, Pallas kernels for 0% -> 0%
where the time goes in v7:
time: 126 us; the launch traced here: 125 us
  blocking collectives  57.4 us (46%)
  waiting for transfers between devices  33.2 us (26%)
  between operations  13.5 us (11%)
  matrix products  10.5 us (8%)
  starting transfers between devices  4.38 us (3%)
  local copies, waits for them, and re-layouts  4.32 us (3%)
  other arithmetic  2.02 us (2%)
    reduce_scatter x1, waiting for transfers between devices, per_device(): lax.psum_scatter(base_bf, MP, scatter_dimension=1, tiled=True)  33.1 us
    all_to_all x2, blocking collectives, spread_over(): lax.all_to_all(jnp.broadcast_to(block[None], (n,) + block.shape), axis, 0...  28.8 us
    all_gather x1, blocking collectives, per_device(): both = lax.all_gather(both, DP[-1], axis=0, tiled=False)  28.5 us
    dot_general x1, matrix products, per_device(): jnp.dot(hidden_rows, base_weight, preferred_element_type=jnp.float32)  6.47 us
    all_to_all x1, starting transfers between devices, spread_over(): lax.all_to_all(jnp.broadcast_to(block[None], (n,) + block.shape), axis, 0...  4.37 us
    dot_general x1, matrix products, per_device(): jnp.dot(placed.reshape(row_count, holders * rank), up_w.reshape(holders *...  2.68 us
  transfers between devices with their start and end apart: 3, of which 1 were waited for; matrix products, arithmetic and copies ran while one was open for 5% of the time, Pallas kernels for 0%

profile of v7, /device:TPU:1, one launch (start us, length us, event | category | flops | bytes accessed | tf_op | source)
XLA Modules:
  0.0 125.2 jit_solution(12609821973767358713)
XLA Ops:
  6.5 0.0 copy-start
  6.5 0.0 reduce-scatter.2.cloned.1.call-start
  6.5 1.0 copy-done
  7.6 6.5 %convolution_convert_fusion = bf16[512,4096]{1,0:T(8,128)(2,1)} fusion(bf16[512,512]{1,0:T(8,128)(2,1)S(1)} %copy-done, bf16[512,4096]{1,0:T(8,128)(2,1)} %param.7), kind=kOutput, calls=%fused_computation | convolution fusion | flops 2149580800 | bytes 8912896 | tf_op jit(solution)/shard_map/dot_general | solution.py:47
  14.0 0.0 copy-start.1
  14.1 0.0 copy-start.2
  14.1 0.0 reduce-scatter.2.cloned.1.call-update
  14.1 0.8 copy-done.1
  14.9 0.0 copy-done.2
  14.9 28.5 %all-gather = bf16[512,768]{1,0:T(8,128)(2,1)S(1)} all-gather(bf16[64,768]{1,0:T(8,128)(2,1)S(1)} %pad_maximum_fusion), channel_id=2, replica_groups=mesh['dp0'=4,'dp2'=8,'mp1'=8,'mp3'=2] {'dp2'}, dimensions={0}, use_global_device_ids=true | all-gather | bytes 884736 | tf_op jit(solution)/shard_map/all_gather | solution.py:40
  43.5 0.0 copy-start.3
  43.5 0.0 copy-start.4
  43.5 1.6 %broadcast_in_dim.74 = bf16[4,8,1,64,512]{4,3,2,1,0:T(8,128)(2,1)} broadcast(bf16[8,64,512]{2,1,0:T(8,128)(2,1)S(1)} %slice_bitcast_fusion), dimensions={1,3,4} | broadcast | bytes 2621440 | tf_op jit(solution)/shard_map/broadcast_in_dim | solution.py:10
  45.1 4.4 %all-to-all-start = ((bf16[4,8,1,64,512]{4,3,2,1,0:T(8,128)(2,1)}), bf16[4,8,1,64,512]{4,3,2,1,0:T(8,128)(2,1)S(1)}, u32[]{:S(2)}, u32[]{:S(2)}) async-start(bf16[4,8,1,64,512]{4,3,2,1,0:T(8,128)(2,1)} %broadcast_in_dim.74), calls=%async_computation.1 | async-start | bytes 4194304 | tf_op jit(solution)/shard_map/all_to_all | solution.py:10
  49.4 0.0 all-gather.4.cloned.1.call-start
  49.4 0.7 slice.8
  50.2 0.0 copy-done.3
  50.2 0.0 copy-done.4
  50.2 0.1 select_reduce_fusion.1
  50.3 33.1 %reduce-scatter.2.cloned.1.call-done = bf16[512,256]{1,0:T(8,128)(2,1)} async-done(((bf16[512,4096]{1,0:T(8,128)(2,1)}), bf16[512,256]{1,0:T(8,128)(2,1)}) %reduce-scatter.2.cloned.1.call-update) | async-done | bytes 262160 | tf_op jit(solution)/shard_map/reduce_scatter | solution.py:49
  83.4 1.0 convert_element_type.25
  84.4 0.0 all-gather.4.cloned.1.call-update
  84.4 0.0 all-to-all-done
  84.4 1.3 %fusion.3 = f32[2048,512]{1,0:T(8,128)S(1)} fusion(bf16[512,2048]{0,1:T(8,128)(2,1)S(1)} %bitcast.24, bf16[512,512]{1,0:T(8,128)(2,1)S(1)} %copy-done), kind=kOutput, calls=%fused_computation.12 | convolution fusion | flops 1073741824 | bytes 6815744 | tf_op jit(solution)/shard_map/dot_general | solution.py:57
  85.8 0.6 select_reduce_fusion
  86.4 22.3 %all_to_all.15 = bf16[8,1,512,64]{2,3,1,0:T(8,128)(2,1)S(1)} all-to-all(bf16[8,1,512,64]{2,3,1,0:T(8,128)(2,1)S(1)} %broadcast_in_dim.76), channel_id=1, replica_groups=mesh['dp0'=4,'dp2'=8,'mp1'=8,'mp3'=2] {'mp1'}, dimensions={0} | all-to-all | bytes 1048576 | tf_op jit(solution)/shard_map/all_to_all | solution.py:10
  108.7 0.1 broadcast_in_dim.78
  108.8 6.6 %all_to_all.16 = bf16[2,8,1,512,64]{3,4,2,1,0:T(8,128)(2,1)S(1)} all-to-all(bf16[2,8,1,512,64]{3,4,2,1,0:T(8,128)(2,1)S(1)} %broadcast_in_dim.78), channel_id=1, replica_groups=mesh['dp0'=4,'dp2'=8,'mp1'=8,'mp3'=2] {'mp3'}, dimensions={0} | all-to-all | bytes 2097152 | tf_op jit(solution)/shard_map/all_to_all | solution.py:10
  115.4 0.1 reduce_sum.32
  115.5 0.1 broadcast_select_fusion
  115.7 0.0 all-gather.4.cloned.1.call-done
  115.7 2.7 %fusion.2 = bf16[512,256]{1,0:T(8,128)(2,1)} fusion(f32[512,256]{1,0:T(8,128)S(1)} %convert_element_type.25, bf16[512,2048]{0,1:T(8,128)(2,1)S(1)} %bitcast.28, bf16[2048,256]{1,0:T(8,128)(2,1)} %bitcast.32), kind=kOutput, calls=%fused_computation.6 | convolution fusion | flops 537395200 | bytes 3932160 | tf_op jit(solution)/shard_map/dot_general | solution.py:70
  (4 shorter events, 0.1 us)
Async XLA Ops:
  6.5 1.0 copy-start
  6.5 76.9 %reduce-scatter.2.cloned.1.call-start = ((), (), s32[]{:S(2)}) async-start(), calls=%async_computation.4 | async-start | bytes 4456448 | tf_op jit(solution)/shard_map/reduce_scatter | solution.py:49
  14.0 0.8 copy-start.1
  14.1 0.8 copy-start.2
  43.5 6.7 %copy-start.3 = (s32[512,1]{0,1:T(1,128)S(1)}, s32[512,1]{0,1:T(1,128)}, u32[]{:S(2)}) copy-start(s32[512,1]{0,1:T(1,128)} %param.10) | copy-start | bytes 6148
  43.5 6.7 %copy-start.4 = (s32[32]{0:T(128)S(1)}, s32[32]{0:T(128)}, u32[]{:S(2)}) copy-start(s32[32]{0:T(128)} %param.11) | copy-start | bytes 388
  45.1 39.3 %all-to-all-start = ((bf16[4,8,1,64,512]{4,3,2,1,0:T(8,128)(2,1)}), bf16[4,8,1,64,512]{4,3,2,1,0:T(8,128)(2,1)S(1)}, u32[]{:S(2)}, u32[]{:S(2)}) async-start(bf16[4,8,1,64,512]{4,3,2,1,0:T(8,128)(2,1)} %broadcast_in_dim.74), calls=%async_computation.1 | async-start | bytes 4194304 | tf_op jit(solution)/shard_map/all_to_all | solution.py:10
  49.4 66.3 %all-gather.4.cloned.1.call-start = ((), (), s32[]{:S(2)}) async-start(), calls=%async_computation.5 | async-start | bytes 1310720 | tf_op jit(solution)/shard_map/all_gather | solution.py:54
Sparse Core Ops, SparseCore 0:
  14.2 69.1 reduce-scatter.1
  85.5 29.0 all-gather.3

commit v8 on v7

--- a/solution.py
+++ b/solution.py
@@ -61,7 +61,7 @@
     ).reshape(row_count, holders, rank)
     partial_down = jnp.sum(jnp.where(slot_hot[:, :, None], every, 0.0), axis=1)
     gathered = partial_down.astype(jnp.bfloat16)[None]
-    for axis in MP:
+    for axis in reversed(MP):
         gathered = spread_over(gathered, axis)
     gathered = gathered.reshape(n_mp, row_count, rank)
     down = jnp.sum(gathered.astype(jnp.float32), axis=0).astype(jnp.bfloat16)

time: 126 us -> 129 us (1.024)
  blocking collectives: 57.4 us -> 38.6 us
  waiting for transfers between devices: 33.2 us -> 48.1 us
  starting transfers between devices: 4.38 us -> 10.5 us
    all_to_all x1 -> x2, waiting for transfers between devices: 0.01 us -> 48 us  [spread_over(): lax.all_to_all(jnp.broadcast_to(block[None], (n,) + block.shape), axis, 0...]
    reduce_scatter x1, waiting for transfers between devices: 33.1 us -> 0.01 us  [per_device(): lax.psum_scatter(base_bf, MP, scatter_dimension=1, tiled=True)]
    all_to_all x2 -> x1, blocking collectives: 28.8 us -> 10.1 us  [spread_over(): lax.all_to_all(jnp.broadcast_to(block[None], (n,) + block.shape), axis, 0...]
    all_to_all x1 -> x2, starting transfers between devices: 4.37 us -> 10.4 us  [spread_over(): lax.all_to_all(jnp.broadcast_to(block[None], (n,) + block.shape), axis, 0...]
  transfers between devices with their start and end apart: 3 -> 4, of which waited for: 1 -> 2; matrix products, arithmetic and copies ran while one was open for 5% -> 5% of each run, Pallas kernels for 0% -> 0%
where the time goes in v8:
time: 129 us; the launch traced here: 128 us
  waiting for transfers between devices  48.1 us (37%)
  blocking collectives  38.6 us (30%)
  between operations  13.5 us (10%)
  starting transfers between devices  10.5 us (8%)
  matrix products  10.5 us (8%)
  local copies, waits for them, and re-layouts  5.27 us (4%)
  other arithmetic  2.02 us (2%)
    all_to_all x2, waiting for transfers between devices, spread_over(): lax.all_to_all(jnp.broadcast_to(block[None], (n,) + block.shape), axis, 0...  48 us
    all_gather x1, blocking collectives, per_device(): both = lax.all_gather(both, DP[-1], axis=0, tiled=False)  28.5 us
    all_to_all x2, starting transfers between devices, spread_over(): lax.all_to_all(jnp.broadcast_to(block[None], (n,) + block.shape), axis, 0...  10.4 us
    all_to_all x1, blocking collectives, spread_over(): lax.all_to_all(jnp.broadcast_to(block[None], (n,) + block.shape), axis, 0...  10.1 us
    dot_general x1, matrix products, per_device(): jnp.dot(hidden_rows, base_weight, preferred_element_type=jnp.float32)  6.48 us
    dot_general x1, matrix products, per_device(): jnp.dot(placed.reshape(row_count, holders * rank), up_w.reshape(holders *...  2.69 us
    broadcast_in_dim x4, local copies, waits for them, and re-layouts, spread_over(): jnp.broadcast_to(block[None], (n,) + block.shape)  2.68 us
  transfers between devices with their start and end apart: 4, of which 2 were waited for; matrix products, arithmetic and copies ran while one was open for 5% of the time, Pallas kernels for 0%

profile of v8, /device:TPU:1, one launch (start us, length us, event | category | flops | bytes accessed | tf_op | source)
XLA Modules:
  0.0 128.4 jit_solution(11928453190464533646)
XLA Ops:
  6.5 0.0 copy-start
  6.5 0.0 reduce-scatter.2.cloned.1.call-start
  6.5 1.0 copy-done
  7.6 6.5 %convolution_convert_fusion = bf16[512,4096]{1,0:T(8,128)(2,1)} fusion(bf16[512,512]{1,0:T(8,128)(2,1)S(1)} %copy-done, bf16[512,4096]{1,0:T(8,128)(2,1)} %param.7), kind=kOutput, calls=%fused_computation | convolution fusion | flops 2149580800 | bytes 8912896 | tf_op jit(solution)/shard_map/dot_general | solution.py:47
  14.1 0.0 copy-start.1
  14.1 0.0 copy-start.2
  14.1 0.0 reduce-scatter.2.cloned.1.call-update
  14.1 0.8 copy-done.1
  14.9 0.0 copy-done.2
  14.9 0.0 copy-start.3
  14.9 0.0 copy-start.4
  14.9 28.5 %all-gather = bf16[512,768]{1,0:T(8,128)(2,1)S(1)} all-gather(bf16[64,768]{1,0:T(8,128)(2,1)S(1)} %pad_maximum_fusion), channel_id=2, replica_groups=mesh['dp0'=4,'dp2'=8,'mp1'=8,'mp3'=2] {'dp2'}, dimensions={0}, use_global_device_ids=true | all-gather | bytes 884736 | tf_op jit(solution)/shard_map/all_gather | solution.py:40
  43.5 1.6 %broadcast_in_dim.74 = bf16[4,8,1,64,512]{4,3,2,1,0:T(8,128)(2,1)} broadcast(bf16[8,64,512]{2,1,0:T(8,128)(2,1)S(1)} %slice_bitcast_fusion), dimensions={1,3,4} | broadcast | bytes 2621440 | tf_op jit(solution)/shard_map/broadcast_in_dim | solution.py:10
  45.1 4.4 %all-to-all-start = ((bf16[4,8,1,64,512]{4,3,2,1,0:T(8,128)(2,1)}), bf16[4,8,1,64,512]{4,3,2,1,0:T(8,128)(2,1)S(1)}, u32[]{:S(2)}, u32[]{:S(2)}) async-start(bf16[4,8,1,64,512]{4,3,2,1,0:T(8,128)(2,1)} %broadcast_in_dim.74), calls=%async_computation.1 | async-start | bytes 4194304 | tf_op jit(solution)/shard_map/all_to_all | solution.py:10
  49.5 0.0 copy-done.3
  49.5 0.0 copy-done.4
  49.5 0.1 select_reduce_fusion.1
  49.6 20.6 %all-to-all-done = bf16[4,8,1,64,512]{4,3,2,1,0:T(8,128)(2,1)S(1)} async-done(((bf16[4,8,1,64,512]{4,3,2,1,0:T(8,128)(2,1)}), bf16[4,8,1,64,512]{4,3,2,1,0:T(8,128)(2,1)S(1)}, u32[]{:S(2)}, u32[]{:S(2)}) %all-to-all-start) | async-done | bytes 2097184 | tf_op jit(solution)/shard_map/all_to_all | solution.py:10
  70.1 1.3 %fusion.3 = f32[2048,512]{1,0:T(8,128)S(1)} fusion(bf16[512,2048]{0,1:T(8,128)(2,1)S(1)} %bitcast.24, bf16[512,512]{1,0:T(8,128)(2,1)S(1)} %copy-done), kind=kOutput, calls=%fused_computation.12 | convolution fusion | flops 1073741824 | bytes 6815744 | tf_op jit(solution)/shard_map/dot_general | solution.py:57
  71.5 0.6 select_reduce_fusion
  72.2 10.1 %all_to_all.15 = bf16[2,1,512,64]{2,3,1,0:T(8,128)(2,1)S(1)} all-to-all(bf16[2,1,512,64]{2,3,1,0:T(8,128)(2,1)S(1)} %broadcast_in_dim.76), channel_id=1, replica_groups=mesh['dp0'=4,'dp2'=8,'mp1'=8,'mp3'=2] {'mp3'}, dimensions={0} | all-to-all | bytes 262144 | tf_op jit(solution)/shard_map/all_to_all | solution.py:10
  82.2 1.1 broadcast_in_dim.78
  83.3 6.0 %all-to-all-start.2 = ((bf16[8,2,1,512,64]{3,4,2,1,0:T(8,128)(2,1)}), bf16[8,2,1,512,64]{3,4,2,1,0:T(8,128)(2,1)S(1)}, u32[]{:S(2)}, u32[]{:S(2)}) async-start(bf16[8,2,1,512,64]{3,4,2,1,0:T(8,128)(2,1)} %broadcast_in_dim.78), calls=%async_computation.3 | async-start | bytes 2097152 | tf_op jit(solution)/shard_map/all_to_all | solution.py:10
  89.3 0.0 all-gather.4.cloned.1.call-start
  89.4 0.7 slice.8
  90.1 0.0 reduce-scatter.2.cloned.1.call-done
  90.1 1.0 convert_element_type.25
  91.1 0.0 all-gather.4.cloned.1.call-update
  91.1 27.5 %all-to-all-done.2 = bf16[8,2,1,512,64]{3,4,2,1,0:T(8,128)(2,1)S(1)} async-done(((bf16[8,2,1,512,64]{3,4,2,1,0:T(8,128)(2,1)}), bf16[8,2,1,512,64]{3,4,2,1,0:T(8,128)(2,1)S(1)}, u32[]{:S(2)}, u32[]{:S(2)}) %all-to-all-start.2) | async-done | bytes 1048608 | tf_op jit(solution)/shard_map/all_to_all | solution.py:10
  118.6 0.1 reduce_sum.32
  118.7 0.1 broadcast_select_fusion
  118.9 0.0 all-gather.4.cloned.1.call-done
  118.9 2.7 %fusion.2 = bf16[512,256]{1,0:T(8,128)(2,1)} fusion(f32[512,256]{1,0:T(8,128)S(1)} %convert_element_type.25, bf16[512,2048]{0,1:T(8,128)(2,1)S(1)} %bitcast.27, bf16[2048,256]{1,0:T(8,128)(2,1)} %bitcast.32), kind=kOutput, calls=%fused_computation.6 | convolution fusion | flops 537395200 | bytes 3932160 | tf_op jit(solution)/shard_map/dot_general | solution.py:70
  (4 shorter events, 0.1 us)
Async XLA Ops:
  6.5 1.0 copy-start
  6.5 83.6 %reduce-scatter.2.cloned.1.call-start = ((), (), s32[]{:S(2)}) async-start(), calls=%async_computation.4 | async-start | bytes 4456448 | tf_op jit(solution)/shard_map/reduce_scatter | solution.py:49
  14.1 0.8 copy-start.1
  14.1 0.8 copy-start.2
  14.9 34.5 %copy-start.3 = (s32[512,1]{0,1:T(1,128)S(1)}, s32[512,1]{0,1:T(1,128)}, u32[]{:S(2)}) copy-start(s32[512,1]{0,1:T(1,128)} %param.10) | copy-start | bytes 6148
  14.9 34.5 %copy-start.4 = (s32[32]{0:T(128)S(1)}, s32[32]{0:T(128)}, u32[]{:S(2)}) copy-start(s32[32]{0:T(128)} %param.11) | copy-start | bytes 388
  45.1 25.1 %all-to-all-start = ((bf16[4,8,1,64,512]{4,3,2,1,0:T(8,128)(2,1)}), bf16[4,8,1,64,512]{4,3,2,1,0:T(8,128)(2,1)S(1)}, u32[]{:S(2)}, u32[]{:S(2)}) async-start(bf16[4,8,1,64,512]{4,3,2,1,0:T(8,128)(2,1)} %broadcast_in_dim.74), calls=%async_computation.1 | async-start | bytes 4194304 | tf_op jit(solution)/shard_map/all_to_all | solution.py:10
  83.3 35.3 %all-to-all-start.2 = ((bf16[8,2,1,512,64]{3,4,2,1,0:T(8,128)(2,1)}), bf16[8,2,1,512,64]{3,4,2,1,0:T(8,128)(2,1)S(1)}, u32[]{:S(2)}, u32[]{:S(2)}) async-start(bf16[8,2,1,512,64]{3,4,2,1,0:T(8,128)(2,1)} %broadcast_in_dim.78), calls=%async_computation.3 | async-start | bytes 2097152 | tf_op jit(solution)/shard_map/all_to_all | solution.py:10
  89.3 29.6 %all-gather.4.cloned.1.call-start = ((), (), s32[]{:S(2)}) async-start(), calls=%async_computation.5 | async-start | bytes 1310720 | tf_op jit(solution)/shard_map/all_gather | solution.py:54
Sparse Core Ops, SparseCore 0:
  14.2 69.1 reduce-scatter.1
  92.3 25.4 all-gather.3

commit v9 on v7

--- a/solution.py
+++ b/solution.py
@@ -2,12 +2,41 @@
 import jax.numpy as jnp
 import numpy as np
 from jax import lax
+from jax.experimental import pallas as pl
+from jax.experimental.pallas import tpu as pltpu
 from jax.sharding import Mesh, PartitionSpec as P
 
 
 def spread_over(block, axis):
     n = lax.axis_size(axis)
     return lax.all_to_all(jnp.broadcast_to(block[None], (n,) + block.shape), axis, 0, 0, tiled=False)
+
+
+def _product_block(x_ref, w_ref, o_ref):
+    o_ref[...] = jnp.dot(x_ref[...], w_ref[...], preferred_element_type=jnp.float32).astype(
+        o_ref.dtype
+    )
+
+
+def base_product(x, w, block=1024):
+    rows, inner = x.shape
+    cols = w.shape[1]
+    block = block if cols % block == 0 else cols
+    return pl.pallas_call(
+        _product_block,
+        grid=(cols // block,),
+        in_specs=[
+            pl.BlockSpec((rows, inner), lambda j: (0, 0)),
+            pl.BlockSpec((inner, block), lambda j: (0, j)),
+        ],
+        out_specs=pl.BlockSpec((rows, block), lambda j: (0, j)),
+        out_shape=jax.ShapeDtypeStruct((rows, cols), jnp.bfloat16),
+        cost_estimate=pl.CostEstimate(
+            flops=2 * rows * inner * cols,
+            transcendentals=0,
+            bytes_accessed=2 * (rows * inner + inner * cols + rows * cols),
+        ),
+    )(x, w)
 
 
 def split_axis(mesh, name):
@@ -44,8 +73,7 @@
         down_w = spread_over(down_w, axis)
     down_w = down_w.reshape(holders, rank, feat_width)
 
-    base_terms = jnp.dot(hidden_rows, base_weight, preferred_element_type=jnp.float32)
-    base_bf = base_terms.astype(jnp.bfloat16)
+    base_bf = base_product(hidden_rows, base_weight)
     base_total = lax.psum_scatter(base_bf, MP, scatter_dimension=1, tiled=True).astype(
         jnp.float32
     )

time: 126 us -> 124 us (0.984)
  matrix products: 10.5 us -> 4.03 us
  Pallas kernels: 0 us -> 6.28 us
    dot_general x1 -> x0, matrix products: 6.47 us -> none  [per_device(): jnp.dot(hidden_rows, base_weight, preferred_element_type=jnp.float32)]
    pallas_call x0 -> x1, Pallas kernels: none -> 6.28 us  [base_product(): pl.pallas_call(_product_block, grid=(cols // block,), in_specs=[pl.BlockS...]
where the time goes in v9:
time: 124 us
  blocking collectives  57.4 us (46%)
  waiting for transfers between devices  33 us (27%)
  between operations  13.5 us (11%)
  Pallas kernels  6.28 us (5%)
  starting transfers between devices  4.51 us (4%)
  matrix products  4.03 us (3%)
  local copies, waits for them, and re-layouts  3.29 us (3%)
  other arithmetic  2.02 us (2%)
    reduce_scatter x1, waiting for transfers between devices, per_device(): lax.psum_scatter(base_bf, MP, scatter_dimension=1, tiled=True)  33 us
    all_to_all x2, blocking collectives, spread_over(): lax.all_to_all(jnp.broadcast_to(block[None], (n,) + block.shape), axis, 0...  28.8 us
    all_gather x1, blocking collectives, per_device(): both = lax.all_gather(both, DP[-1], axis=0, tiled=False)  28.5 us
    pallas_call x1, Pallas kernels, base_product(): pl.pallas_call(_product_block, grid=(cols // block,), in_specs=[pl.BlockS...  6.28 us
    all_to_all x1, starting transfers between devices, spread_over(): lax.all_to_all(jnp.broadcast_to(block[None], (n,) + block.shape), axis, 0...  4.5 us
    dot_general x1, matrix products, per_device(): jnp.dot(placed.reshape(row_count, holders * rank), up_w.reshape(holders *...  2.69 us
  transfers between devices with their start and end apart: 3, of which 1 were waited for; matrix products, arithmetic and copies ran while one was open for 5% of the time, Pallas kernels for 0%

profile of v9, /device:TPU:1, one launch (start us, length us, event | category | flops | bytes accessed | tf_op | source)
XLA Modules:
  0.0 124.0 jit_solution(9848678983869317249)
XLA Ops:
  6.5 0.0 reduce-scatter.2.cloned.1.call-start
  6.5 6.3 %shard_map.64 = bf16[512,4096]{1,0:T(8,128)(2,1)} custom-call(bf16[512,512]{1,0:T(8,128)(2,1)} %x_ref.1, bf16[512,4096]{1,0:T(8,128)(2,1)} %w_ref.1), custom_call_target="tpu_custom_call" | custom-call | flops 2147483648 | bytes 8912896 | tf_op jit(solution)/shard_map/pallas_call | solution.py:25
  12.8 0.0 copy-start.1
  12.8 0.0 copy-start.2
  12.8 0.0 reduce-scatter.2.cloned.1.call-update
  12.8 0.8 copy-done.1
  13.7 0.0 copy-done.2
  13.7 28.5 %all-gather = bf16[512,768]{1,0:T(8,128)(2,1)S(1)} all-gather(bf16[64,768]{1,0:T(8,128)(2,1)S(1)} %pad_maximum_fusion), channel_id=2, replica_groups=mesh['dp0'=4,'dp2'=8,'mp1'=8,'mp3'=2] {'dp2'}, dimensions={0}, use_global_device_ids=true | all-gather | bytes 884736 | tf_op jit(solution)/shard_map/all_gather | solution.py:69
  42.3 1.6 %broadcast_in_dim.74 = bf16[4,8,1,64,512]{4,3,2,1,0:T(8,128)(2,1)} broadcast(bf16[8,64,512]{2,1,0:T(8,128)(2,1)S(1)} %slice_bitcast_fusion), dimensions={1,3,4} | broadcast | bytes 2621440 | tf_op jit(solution)/shard_map/broadcast_in_dim | solution.py:12
  43.8 0.0 copy-start.3
  43.8 0.0 copy-start.4
  43.8 0.0 copy-start
  43.8 4.5 %all-to-all-start = ((bf16[4,8,1,64,512]{4,3,2,1,0:T(8,128)(2,1)}), bf16[4,8,1,64,512]{4,3,2,1,0:T(8,128)(2,1)S(1)}, u32[]{:S(2)}, u32[]{:S(2)}) async-start(bf16[4,8,1,64,512]{4,3,2,1,0:T(8,128)(2,1)} %broadcast_in_dim.74), calls=%async_computation.1 | async-start | bytes 4194304 | tf_op jit(solution)/shard_map/all_to_all | solution.py:12
  48.3 0.0 all-gather.4.cloned.1.call-start
  48.3 0.7 slice.8
  49.1 0.0 copy-done.3
  49.1 0.0 copy-done.4
  49.1 0.1 select_reduce_fusion.1
  49.2 33.0 %reduce-scatter.2.cloned.1.call-done = bf16[512,256]{1,0:T(8,128)(2,1)} async-done(((bf16[512,4096]{1,0:T(8,128)(2,1)}), bf16[512,256]{1,0:T(8,128)(2,1)}) %reduce-scatter.2.cloned.1.call-update) | async-done | bytes 262160 | tf_op jit(solution)/shard_map/reduce_scatter | solution.py:77
  82.2 1.0 convert_element_type.21
  83.1 0.0 all-gather.4.cloned.1.call-update
  83.2 0.0 all-to-all-done
  83.2 0.0 copy-done
  83.2 1.3 %fusion.3 = f32[2048,512]{1,0:T(8,128)S(1)} fusion(bf16[512,2048]{0,1:T(8,128)(2,1)S(1)} %bitcast.22, bf16[512,512]{1,0:T(8,128)(2,1)S(1)} %copy-done), kind=kOutput, calls=%fused_computation.11 | convolution fusion | flops 1073741824 | bytes 6815744 | tf_op jit(solution)/shard_map/dot_general | solution.py:85
  84.5 0.6 select_reduce_fusion
  85.2 22.2 %all_to_all.15 = bf16[8,1,512,64]{2,3,1,0:T(8,128)(2,1)S(1)} all-to-all(bf16[8,1,512,64]{2,3,1,0:T(8,128)(2,1)S(1)} %broadcast_in_dim.76), channel_id=1, replica_groups=mesh['dp0'=4,'dp2'=8,'mp1'=8,'mp3'=2] {'mp1'}, dimensions={0} | all-to-all | bytes 1048576 | tf_op jit(solution)/shard_map/all_to_all | solution.py:12
  107.5 0.1 broadcast_in_dim.78
  107.6 6.6 %all_to_all.16 = bf16[2,8,1,512,64]{3,4,2,1,0:T(8,128)(2,1)S(1)} all-to-all(bf16[2,8,1,512,64]{3,4,2,1,0:T(8,128)(2,1)S(1)} %broadcast_in_dim.78), channel_id=1, replica_groups=mesh['dp0'=4,'dp2'=8,'mp1'=8,'mp3'=2] {'mp3'}, dimensions={0} | all-to-all | bytes 2097152 | tf_op jit(solution)/shard_map/all_to_all | solution.py:12
  114.1 0.1 reduce_sum.32
  114.3 0.1 broadcast_select_fusion
  114.4 0.0 all-gather.4.cloned.1.call-done
  114.5 2.7 %fusion.2 = bf16[512,256]{1,0:T(8,128)(2,1)} fusion(f32[512,256]{1,0:T(8,128)S(1)} %convert_element_type.21, bf16[512,2048]{0,1:T(8,128)(2,1)S(1)} %bitcast.26, bf16[2048,256]{1,0:T(8,128)(2,1)} %bitcast.30), kind=kOutput, calls=%fused_computation.5 | convolution fusion | flops 537395200 | bytes 3932160 | tf_op jit(solution)/shard_map/dot_general | solution.py:98
  (4 shorter events, 0.1 us)
Async XLA Ops:
  6.5 75.6 %reduce-scatter.2.cloned.1.call-start = ((), (), s32[]{:S(2)}) async-start(), calls=%async_computation.4 | async-start | bytes 4456448 | tf_op jit(solution)/shard_map/reduce_scatter | solution.py:77
  12.8 0.8 copy-start.1
  12.8 0.8 copy-start.2
  43.8 5.2 %copy-start.3 = (s32[512,1]{0,1:T(1,128)S(1)}, s32[512,1]{0,1:T(1,128)}, u32[]{:S(2)}) copy-start(s32[512,1]{0,1:T(1,128)} %param.10) | copy-start | bytes 6148
  43.8 5.2 %copy-start.4 = (s32[32]{0:T(128)S(1)}, s32[32]{0:T(128)}, u32[]{:S(2)}) copy-start(s32[32]{0:T(128)} %param.11) | copy-start | bytes 388
  43.8 39.3 %copy-start = (bf16[512,512]{1,0:T(8,128)(2,1)S(1)}, bf16[512,512]{1,0:T(8,128)(2,1)}, u32[]{:S(2)}) copy-start(bf16[512,512]{1,0:T(8,128)(2,1)} %x_ref.1) | copy-start | bytes 1572868
  43.8 39.3 %all-to-all-start = ((bf16[4,8,1,64,512]{4,3,2,1,0:T(8,128)(2,1)}), bf16[4,8,1,64,512]{4,3,2,1,0:T(8,128)(2,1)S(1)}, u32[]{:S(2)}, u32[]{:S(2)}) async-start(bf16[4,8,1,64,512]{4,3,2,1,0:T(8,128)(2,1)} %broadcast_in_dim.74), calls=%async_computation.1 | async-start | bytes 4194304 | tf_op jit(solution)/shard_map/all_to_all | solution.py:12
  48.3 66.1 %all-gather.4.cloned.1.call-start = ((), (), s32[]{:S(2)}) async-start(), calls=%async_computation.5 | async-start | bytes 1310720 | tf_op jit(solution)/shard_map/all_gather | solution.py:82
Sparse Core Ops, SparseCore 0:
  13.0 69.1 reduce-scatter.1
  84.3 29.0 all-gather.3

commit v10 on v9

--- a/solution.py
+++ b/solution.py
@@ -73,10 +73,10 @@
         down_w = spread_over(down_w, axis)
     down_w = down_w.reshape(holders, rank, feat_width)
 
-    base_bf = base_product(hidden_rows, base_weight)
-    base_total = lax.psum_scatter(base_bf, MP, scatter_dimension=1, tiled=True).astype(
-        jnp.float32
-    )
+    base_t = lax.dot_general(
+        base_weight, hidden_rows, (((0,), (1,)), ((), ())), preferred_element_type=jnp.float32
+    ).astype(jnp.bfloat16)
+    base_total = lax.psum_scatter(base_t, MP, scatter_dimension=0, tiled=True).astype(jnp.float32)
     up_w, base_total = lax.optimization_barrier((up_w, base_total))
     for axis in reversed(DP[:-1]):
         up_w = lax.all_gather(up_w, axis, axis=0, tiled=False)
@@ -100,7 +100,7 @@
         up_w.reshape(holders * rank, out_width),
         preferred_element_type=jnp.float32,
     ).astype(jnp.bfloat16)
-    return (base_total + lift.astype(jnp.float32)).astype(jnp.bfloat16)
+    return (base_total.T + lift.astype(jnp.float32)).astype(jnp.bfloat16)
 
 
 def coordinate(device, c):

time: 124 us -> 126 us (1.016)
  Pallas kernels: 6.28 us -> 0 us
  matrix products: 4.03 us -> 9.85 us
  local copies, waits for them, and re-layouts: 3.29 us -> 5.16 us
    dot_general x0 -> x1, matrix products: none -> 6.53 us  [per_device(): lax.dot_general(base_weight, hidden_rows, (((0,), (1,)), ((), ())), prefe...]
    pallas_call x1 -> x0, Pallas kernels: 6.28 us -> none  [base_product(): pl.pallas_call(_product_block, grid=(cols // block,), in_specs=[pl.BlockS...]
where the time goes in v10:
time: 126 us; the launch traced here: 125 us
  blocking collectives  57.3 us (45%)
  waiting for transfers between devices  33.2 us (26%)
  between operations  13.5 us (11%)
  matrix products  9.85 us (8%)
  local copies, waits for them, and re-layouts  5.16 us (4%)
  starting transfers between devices  4.38 us (3%)
  other arithmetic  2.04 us (2%)
    reduce_scatter x1, waiting for transfers between devices, per_device(): lax.psum_scatter(base_t, MP, scatter_dimension=0, tiled=True)  33.1 us
    all_to_all x2, blocking collectives, spread_over(): lax.all_to_all(jnp.broadcast_to(block[None], (n,) + block.shape), axis, 0...  28.8 us
    all_gather x1, blocking collectives, per_device(): both = lax.all_gather(both, DP[-1], axis=0, tiled=False)  28.6 us
    dot_general x1, matrix products, per_device(): lax.dot_general(base_weight, hidden_rows, (((0,), (1,)), ((), ())), prefe...  6.53 us
    all_to_all x1, starting transfers between devices, spread_over(): lax.all_to_all(jnp.broadcast_to(block[None], (n,) + block.shape), axis, 0...  4.37 us
  transfers between devices with their start and end apart: 3, of which 1 were waited for; matrix products, arithmetic and copies ran while one was open for 5% of the time, Pallas kernels for 0%

profile of v10, /device:TPU:1, one launch (start us, length us, event | category | flops | bytes accessed | tf_op | source)
XLA Modules:
  0.0 125.4 jit_solution(9254497406300166426)
XLA Ops:
  6.5 0.0 copy-start
  6.5 0.0 reduce-scatter.2.cloned.1.call-start
  6.5 1.0 copy-done
  7.6 6.5 %convolution_convert_fusion = bf16[4096,512]{1,0:T(8,128)(2,1)} fusion(bf16[512,4096]{1,0:T(8,128)(2,1)} %param.7, bf16[512,512]{1,0:T(8,128)(2,1)S(1)} %copy-done), kind=kOutput, calls=%fused_computation | convolution fusion | flops 2149580800 | bytes 8912896 | tf_op jit(solution)/shard_map/dot_general | solution.py:76
  14.1 0.0 copy-start.1
  14.1 0.0 copy-start.2
  14.1 0.0 reduce-scatter.2.cloned.1.call-update
  14.1 0.8 copy-done.1
  14.9 0.0 copy-done.2
  15.0 28.6 %all-gather = bf16[512,768]{1,0:T(8,128)(2,1)S(1)} all-gather(bf16[64,768]{1,0:T(8,128)(2,1)S(1)} %pad_maximum_fusion), channel_id=2, replica_groups=mesh['dp0'=4,'dp2'=8,'mp1'=8,'mp3'=2] {'dp2'}, dimensions={0}, use_global_device_ids=true | all-gather | bytes 884736 | tf_op jit(solution)/shard_map/all_gather | solution.py:69
  43.5 0.0 copy-start.3
  43.5 0.0 copy-start.4
  43.6 1.6 %broadcast_in_dim.74 = bf16[4,8,1,64,512]{4,3,2,1,0:T(8,128)(2,1)} broadcast(bf16[8,64,512]{2,1,0:T(8,128)(2,1)S(1)} %slice_bitcast_fusion), dimensions={1,3,4} | broadcast | bytes 2621440 | tf_op jit(solution)/shard_map/broadcast_in_dim | solution.py:12
  45.1 4.4 %all-to-all-start = ((bf16[4,8,1,64,512]{4,3,2,1,0:T(8,128)(2,1)}), bf16[4,8,1,64,512]{4,3,2,1,0:T(8,128)(2,1)S(1)}, u32[]{:S(2)}, u32[]{:S(2)}) async-start(bf16[4,8,1,64,512]{4,3,2,1,0:T(8,128)(2,1)} %broadcast_in_dim.74), calls=%async_computation.1 | async-start | bytes 4194304 | tf_op jit(solution)/shard_map/all_to_all | solution.py:12
  49.5 0.0 all-gather.4.cloned.1.call-start
  49.5 0.7 slice.8
  50.2 0.0 copy-done.3
  50.2 0.0 copy-done.4
  50.2 0.1 select_reduce_fusion.1
  50.3 33.1 %reduce-scatter.2.cloned.1.call-done = bf16[256,512]{1,0:T(8,128)(2,1)} async-done(((bf16[4096,512]{1,0:T(8,128)(2,1)}), bf16[256,512]{1,0:T(8,128)(2,1)}) %reduce-scatter.2.cloned.1.call-update) | async-done | bytes 262160 | tf_op jit(solution)/shard_map/reduce_scatter | solution.py:79
  83.4 1.0 convert_element_type.25
  84.5 0.0 all-gather.4.cloned.1.call-update
  84.5 0.0 all-to-all-done
  84.5 1.3 %fusion.3 = f32[2048,512]{1,0:T(8,128)S(1)} fusion(bf16[512,2048]{0,1:T(8,128)(2,1)S(1)} %bitcast.26, bf16[512,512]{1,0:T(8,128)(2,1)S(1)} %copy-done), kind=kOutput, calls=%fused_computation.12 | convolution fusion | flops 1073741824 | bytes 6815744 | tf_op jit(solution)/shard_map/dot_general | solution.py:85
  85.8 0.6 select_reduce_fusion
  86.5 22.2 %all_to_all.15 = bf16[8,1,512,64]{2,3,1,0:T(8,128)(2,1)S(1)} all-to-all(bf16[8,1,512,64]{2,3,1,0:T(8,128)(2,1)S(1)} %broadcast_in_dim.76), channel_id=1, replica_groups=mesh['dp0'=4,'dp2'=8,'mp1'=8,'mp3'=2] {'mp1'}, dimensions={0} | all-to-all | bytes 1048576 | tf_op jit(solution)/shard_map/all_to_all | solution.py:12
  108.8 0.1 broadcast_in_dim.78
  108.9 6.6 %all_to_all.16 = bf16[2,8,1,512,64]{3,4,2,1,0:T(8,128)(2,1)S(1)} all-to-all(bf16[2,8,1,512,64]{3,4,2,1,0:T(8,128)(2,1)S(1)} %broadcast_in_dim.78), channel_id=1, replica_groups=mesh['dp0'=4,'dp2'=8,'mp1'=8,'mp3'=2] {'mp3'}, dimensions={0} | all-to-all | bytes 2097152 | tf_op jit(solution)/shard_map/all_to_all | solution.py:12
  115.4 0.1 reduce_sum.32
  115.6 0.1 broadcast_select_fusion
  115.7 0.0 all-gather.4.cloned.1.call-done
  115.8 2.0 %fusion.2 = bf16[512,256]{0,1:T(8,128)(2,1)S(1)} fusion(bf16[512,2048]{0,1:T(8,128)(2,1)S(1)} %bitcast.30, bf16[2048,256]{1,0:T(8,128)(2,1)} %bitcast.34, f32[256,512]{1,0:T(8,128)S(1)} %convert_element_type.25), kind=kOutput, calls=%fused_computation.6 | convolution fusion | flops 537395200 | bytes 3932160 | tf_op jit(solution)/shard_map/dot_general | solution.py:98
  117.7 0.8 copy.12
  (4 shorter events, 0.1 us)
Async XLA Ops:
  6.5 1.0 copy-start
  6.5 76.9 %reduce-scatter.2.cloned.1.call-start = ((), (), s32[]{:S(2)}) async-start(), calls=%async_computation.4 | async-start | bytes 4456448 | tf_op jit(solution)/shard_map/reduce_scatter | solution.py:79
  14.1 0.8 copy-start.1
  14.1 0.8 copy-start.2
  43.5 6.7 %copy-start.3 = (s32[512,1]{0,1:T(1,128)S(1)}, s32[512,1]{0,1:T(1,128)}, u32[]{:S(2)}) copy-start(s32[512,1]{0,1:T(1,128)} %param.10) | copy-start | bytes 6148
  43.5 6.7 %copy-start.4 = (s32[32]{0:T(128)S(1)}, s32[32]{0:T(128)}, u32[]{:S(2)}) copy-start(s32[32]{0:T(128)} %param.11) | copy-start | bytes 388
  45.1 39.4 %all-to-all-start = ((bf16[4,8,1,64,512]{4,3,2,1,0:T(8,128)(2,1)}), bf16[4,8,1,64,512]{4,3,2,1,0:T(8,128)(2,1)S(1)}, u32[]{:S(2)}, u32[]{:S(2)}) async-start(bf16[4,8,1,64,512]{4,3,2,1,0:T(8,128)(2,1)} %broadcast_in_dim.74), calls=%async_computation.1 | async-start | bytes 4194304 | tf_op jit(solution)/shard_map/all_to_all | solution.py:12
  49.5 66.3 %all-gather.4.cloned.1.call-start = ((), (), s32[]{:S(2)}) async-start(), calls=%async_computation.5 | async-start | bytes 1310720 | tf_op jit(solution)/shard_map/all_gather | solution.py:82
Sparse Core Ops, SparseCore 0:
  14.3 69.1 reduce-scatter.1
  85.5 29.0 all-gather.3

commit v11 on v9

--- a/solution.py
+++ b/solution.py
@@ -73,10 +73,24 @@
         down_w = spread_over(down_w, axis)
     down_w = down_w.reshape(holders, rank, feat_width)
 
-    base_bf = base_product(hidden_rows, base_weight)
-    base_total = lax.psum_scatter(base_bf, MP, scatter_dimension=1, tiled=True).astype(
-        jnp.float32
-    )
+    if len(MP) == 2:
+        n_y, n_c = lax.axis_size(MP[0]), lax.axis_size(MP[1])
+        base_t = lax.dot_general(
+            base_weight.reshape(feat_width, n_y, n_c, -1),
+            hidden_rows,
+            (((0,), (1,)), ((), ())),
+            preferred_element_type=jnp.float32,
+        ).astype(jnp.bfloat16)
+        base_t = base_t.transpose(1, 0, 2, 3)
+        base_t = lax.all_to_all(base_t, MP[1], 0, 0, tiled=True)
+        base_t = jnp.sum(base_t.astype(jnp.float32), axis=0).astype(jnp.bfloat16)
+        base_t = lax.psum_scatter(base_t, MP[0], scatter_dimension=0, tiled=True)
+        base_total = base_t.reshape(-1, row_count).T.astype(jnp.float32)
+    else:
+        base_bf = base_product(hidden_rows, base_weight)
+        base_total = lax.psum_scatter(base_bf, MP, scatter_dimension=1, tiled=True).astype(
+            jnp.float32
+        )
     up_w, base_total = lax.optimization_barrier((up_w, base_total))
     for axis in reversed(DP[:-1]):
         up_w = lax.all_gather(up_w, axis, axis=0, tiled=False)

time: 124 us -> 131 us (1.056)
  waiting for transfers between devices: 33 us -> 19.6 us
  blocking collectives: 57.4 us -> 67.1 us
  local copies, waits for them, and re-layouts: 3.29 us -> 11.8 us
  Pallas kernels: 6.28 us -> 0 us
  matrix products: 4.03 us -> 8.59 us
  other arithmetic: 2.02 us -> 5.35 us
    reduce_scatter x1, waiting for transfers between devices: 33 us -> 10.2 us  [per_device(): base_t = lax.psum_scatter(base_t, MP[0], scatter_dimension=0, tiled=True)]
    all_to_all x0 -> x1, blocking collectives: none -> 14.7 us  [per_device(): base_t = lax.all_to_all(base_t, MP[1], 0, 0, tiled=True)]
    all_to_all x1, waiting for transfers between devices: 0.01 us -> 9.36 us  [spread_over(): lax.all_to_all(jnp.broadcast_to(block[None], (n,) + block.shape), axis, 0...]
    reshape x0 -> x1, local copies, waits for them, and re-layouts: none -> 6.52 us  [per_device(): base_weight.reshape(feat_width, n_y, n_c, -1)]
    pallas_call x1 -> x0, Pallas kernels: 6.28 us -> none  [base_product(): pl.pallas_call(_product_block, grid=(cols // block,), in_specs=[pl.BlockS...]
    all_gather x1, blocking collectives: 28.5 us -> 22.8 us  [per_device(): both = lax.all_gather(both, DP[-1], axis=0, tiled=False)]
    dot_general x0 -> x1, matrix products: none -> 4.56 us  [per_device(): lax.dot_general(base_weight.reshape(feat_width, n_y, n_c, -1), hidden_row...]
    reduce_sum x0 -> x1, other arithmetic: none -> 3.33 us  [per_device(): base_t = jnp.sum(base_t.astype(jnp.float32), axis=0).astype(jnp.bfloat16)]
  transfers between devices with their start and end apart: 3 -> 3, of which waited for: 1 -> 2; matrix products, arithmetic and copies ran while one was open for 5% -> 5% of each run, Pallas kernels for 0% -> 0%
where the time goes in v11:
time: 131 us; the launch traced here: 130 us
  blocking collectives  67.1 us (51%)
  waiting for transfers between devices  19.6 us (15%)
  between operations  13.5 us (10%)
  local copies, waits for them, and re-layouts  11.8 us (9%)
  matrix products  8.59 us (7%)
  other arithmetic  5.35 us (4%)
  starting transfers between devices  4.06 us (3%)
    all_to_all x2, blocking collectives, spread_over(): lax.all_to_all(jnp.broadcast_to(block[None], (n,) + block.shape), axis, 0...  29.6 us
    all_gather x1, blocking collectives, per_device(): both = lax.all_gather(both, DP[-1], axis=0, tiled=False)  22.8 us
    all_to_all x1, blocking collectives, per_device(): base_t = lax.all_to_all(base_t, MP[1], 0, 0, tiled=True)  14.7 us
    reduce_scatter x1, waiting for transfers between devices, per_device(): base_t = lax.psum_scatter(base_t, MP[0], scatter_dimension=0, tiled=True)  10.2 us
    all_to_all x1, waiting for transfers between devices, spread_over(): lax.all_to_all(jnp.broadcast_to(block[None], (n,) + block.shape), axis, 0...  9.36 us
    reshape x1, local copies, waits for them, and re-layouts, per_device(): base_weight.reshape(feat_width, n_y, n_c, -1)  6.52 us
    dot_general x1, matrix products, per_device(): lax.dot_general(base_weight.reshape(feat_width, n_y, n_c, -1), hidden_row...  4.56 us
    all_to_all x1, starting transfers between devices, spread_over(): lax.all_to_all(jnp.broadcast_to(block[None], (n,) + block.shape), axis, 0...  4.06 us
  transfers between devices with their start and end apart: 3, of which 2 were waited for; matrix products, arithmetic and copies ran while one was open for 5% of the time, Pallas kernels for 0%

profile of v11, /device:TPU:1, one launch (start us, length us, event | category | flops | bytes accessed | tf_op | source)
XLA Modules:
  0.0 130.1 jit_solution(12784574203510512032)
XLA Ops:
  6.5 0.0 copy-start
  6.5 0.0 reduce-scatter.2.cloned.1.call-start
  6.5 6.5 %copy.17 = bf16[512,4096]{0,1:T(8,128)(2,1)} copy(bf16[512,4096]{1,0:T(8,128)(2,1)} %param.7) | data formatting | bytes 8388608 | tf_op jit(solution)/shard_map/reshape | solution.py:79
  13.1 0.0 copy-done
  13.1 4.6 %convert_bitcast_fusion = bf16[2,8,256,512]{3,2,0,1:T(8,128)(2,1)S(1)} fusion(bf16[512,8,2,256]{0,3,2,1:T(8,128)(2,1)} %bitcast.37, bf16[512,512]{1,0:T(8,128)(2,1)S(1)} %copy-done), kind=kOutput, calls=%fused_computation.1 | convolution fusion | flops 2149580800 | bytes 8912896 | tf_op jit(solution)/shard_map/dot_general | solution.py:78
  17.6 0.4 copy.13
  18.0 14.7 %all_to_all.20 = bf16[2,8,256,512]{3,2,1,0:T(8,128)(2,1)} all-to-all(bf16[2,8,256,512]{3,2,1,0:T(8,128)(2,1)S(1)} %copy.13), channel_id=1, replica_groups=mesh['dp0'=4,'dp2'=8,'mp1'=8,'mp3'=2] {'mp3'}, dimensions={0} | all-to-all | bytes 8388608 | tf_op jit(solution)/shard_map/all_to_all | solution.py:85
  32.7 3.3 %reduce_sum.42 = bf16[8,256,512]{2,1,0:T(8,128)(2,1)S(1)} reduce(bf16[2,8,256,512]{3,2,1,0:T(8,128)(2,1)} %all_to_all.20, bf16[]{:T(256)} %constant.2.clone.1), dimensions={0}, to_apply=%region_0.1 | reduce | flops 1048576 | bytes 6291458 | tf_op jit(solution)/shard_map/reduce_sum | solution.py:86
  36.0 0.0 copy-start.1
  36.0 0.0 copy-start.2
  36.0 2.4 %copy.15 = bf16[8,256,512]{1,2,0:T(8,128)(2,1)} copy(bf16[8,256,512]{2,1,0:T(8,128)(2,1)S(1)} %reduce_sum.42) | data formatting | bytes 4194304 | tf_op jit(solution)/shard_map/reduce_sum | solution.py:86
  38.5 0.0 reduce-scatter.2.cloned.1.call-update
  38.5 0.0 copy-done.1
  38.5 0.0 copy-done.2
  38.5 22.8 %all-gather = bf16[512,768]{1,0:T(8,128)(2,1)S(1)} all-gather(bf16[64,768]{1,0:T(8,128)(2,1)S(1)} %pad_maximum_fusion), channel_id=2, replica_groups=mesh['dp0'=4,'dp2'=8,'mp1'=8,'mp3'=2] {'dp2'}, dimensions={0}, use_global_device_ids=true | all-gather | bytes 884736 | tf_op jit(solution)/shard_map/all_gather | solution.py:69
  61.3 0.0 copy-start.3
  61.3 0.0 copy-start.4
  61.4 1.6 %broadcast_in_dim.74 = bf16[4,8,1,64,512]{4,3,2,1,0:T(8,128)(2,1)} broadcast(bf16[8,64,512]{2,1,0:T(8,128)(2,1)S(1)} %slice_bitcast_fusion), dimensions={1,3,4} | broadcast | bytes 2621440 | tf_op jit(solution)/shard_map/broadcast_in_dim | solution.py:12
  63.0 4.1 %all-to-all-start.1 = ((bf16[4,8,1,64,512]{4,3,2,1,0:T(8,128)(2,1)}), bf16[4,8,1,64,512]{4,3,2,1,0:T(8,128)(2,1)S(1)}, u32[]{:S(2)}, u32[]{:S(2)}) async-start(bf16[4,8,1,64,512]{4,3,2,1,0:T(8,128)(2,1)} %broadcast_in_dim.74), calls=%async_computation.2 | async-start | bytes 4194304 | tf_op jit(solution)/shard_map/all_to_all | solution.py:12
  67.0 0.0 all-gather.4.cloned.1.call-start
  67.0 0.7 slice.8
  67.8 0.0 copy-done.3
  67.8 0.0 copy-done.4
  67.8 0.1 select_reduce_fusion.1
  67.9 10.2 %reduce-scatter.2.cloned.1.call-done = bf16[1,256,512]{1,2,0:T(8,128)(2,1)} async-done(((bf16[8,256,512]{1,2,0:T(8,128)(2,1)}), bf16[1,256,512]{1,2,0:T(8,128)(2,1)}) %reduce-scatter.2.cloned.1.call-update) | async-done | bytes 262160 | tf_op jit(solution)/shard_map/reduce_scatter | solution.py:87
  78.1 1.0 convert_bitcast_fusion.1
  79.1 0.0 all-gather.4.cloned.1.call-update
  79.1 9.4 %all-to-all-done.1 = bf16[4,8,1,64,512]{4,3,2,1,0:T(8,128)(2,1)S(1)} async-done(((bf16[4,8,1,64,512]{4,3,2,1,0:T(8,128)(2,1)}), bf16[4,8,1,64,512]{4,3,2,1,0:T(8,128)(2,1)S(1)}, u32[]{:S(2)}, u32[]{:S(2)}) %all-to-all-start.1) | async-done | bytes 2097184 | tf_op jit(solution)/shard_map/all_to_all | solution.py:12
  88.5 1.3 %fusion.4 = f32[2048,512]{1,0:T(8,128)S(1)} fusion(bf16[512,2048]{0,1:T(8,128)(2,1)S(1)} %bitcast.36, bf16[512,512]{1,0:T(8,128)(2,1)S(1)} %copy-done), kind=kOutput, calls=%fused_computation.14 | convolution fusion | flops 1073741824 | bytes 6815744 | tf_op jit(solution)/shard_map/dot_general | solution.py:99
  89.8 0.6 select_reduce_fusion
  90.5 17.1 %all_to_all.21 = bf16[8,1,512,64]{2,3,1,0:T(8,128)(2,1)S(1)} all-to-all(bf16[8,1,512,64]{2,3,1,0:T(8,128)(2,1)S(1)} %broadcast_in_dim.76), channel_id=1, replica_groups=mesh['dp0'=4,'dp2'=8,'mp1'=8,'mp3'=2] {'mp1'}, dimensions={0} | all-to-all | bytes 1048576 | tf_op jit(solution)/shard_map/all_to_all | solution.py:12
  107.6 0.1 broadcast_in_dim.78
  107.7 12.5 %all_to_all.22 = bf16[2,8,1,512,64]{3,4,2,1,0:T(8,128)(2,1)S(1)} all-to-all(bf16[2,8,1,512,64]{3,4,2,1,0:T(8,128)(2,1)S(1)} %broadcast_in_dim.78), channel_id=1, replica_groups=mesh['dp0'=4,'dp2'=8,'mp1'=8,'mp3'=2] {'mp3'}, dimensions={0} | all-to-all | bytes 2097152 | tf_op jit(solution)/shard_map/all_to_all | solution.py:12
  120.2 0.1 reduce_sum.45
  120.4 0.1 broadcast_select_fusion
  120.5 0.0 all-gather.4.cloned.1.call-done
  120.5 2.7 %fusion.2 = bf16[512,256]{1,0:T(8,128)(2,1)} fusion(f32[512,256]{1,0:T(8,128)S(1)} %convert_bitcast_fusion.1, bf16[512,2048]{0,1:T(8,128)(2,1)S(1)} %bitcast.41, bf16[2048,256]{1,0:T(8,128)(2,1)} %bitcast.45), kind=kOutput, calls=%fused_computation.6 | convolution fusion | flops 537395200 | bytes 3932160 | tf_op jit(solution)/shard_map/dot_general | solution.py:112
  (4 shorter events, 0.1 us)
Async XLA Ops:
  6.5 6.5 %copy-start = (bf16[512,512]{1,0:T(8,128)(2,1)S(1)}, bf16[512,512]{1,0:T(8,128)(2,1)}, u32[]{:S(2)}) copy-start(bf16[512,512]{1,0:T(8,128)(2,1)} %param.6) | copy-start | bytes 1572868
  6.5 71.6 %reduce-scatter.2.cloned.1.call-start = ((), (), s32[]{:S(2)}) async-start(), calls=%async_computation.5 | async-start | bytes 2359296 | tf_op jit(solution)/shard_map/reduce_scatter | solution.py:87
  36.0 2.5 %copy-start.1 = (bf16[1,64,512]{2,1,0:T(8,128)(2,1)S(1)}, bf16[1,64,512]{2,1,0:T(8,128)(2,1)}, u32[]{:S(2)}) copy-start(bf16[1,64,512]{2,1,0:T(8,128)(2,1)} %param.8) | copy-start | bytes 196612
  36.0 2.5 %copy-start.2 = (bf16[1,64,256]{2,1,0:T(8,128)(2,1)S(1)}, bf16[1,64,256]{2,1,0:T(8,128)(2,1)}, u32[]{:S(2)}) copy-start(bf16[1,64,256]{2,1,0:T(8,128)(2,1)} %param.9) | copy-start | bytes 98308
  61.3 6.4 %copy-start.3 = (s32[512,1]{0,1:T(1,128)S(1)}, s32[512,1]{0,1:T(1,128)}, u32[]{:S(2)}) copy-start(s32[512,1]{0,1:T(1,128)} %param.10) | copy-start | bytes 6148
  61.3 6.4 %copy-start.4 = (s32[32]{0:T(128)S(1)}, s32[32]{0:T(128)}, u32[]{:S(2)}) copy-start(s32[32]{0:T(128)} %param.11) | copy-start | bytes 388
  63.0 25.5 %all-to-all-start.1 = ((bf16[4,8,1,64,512]{4,3,2,1,0:T(8,128)(2,1)}), bf16[4,8,1,64,512]{4,3,2,1,0:T(8,128)(2,1)S(1)}, u32[]{:S(2)}, u32[]{:S(2)}) async-start(bf16[4,8,1,64,512]{4,3,2,1,0:T(8,128)(2,1)} %broadcast_in_dim.74), calls=%async_computation.2 | async-start | bytes 4194304 | tf_op jit(solution)/shard_map/all_to_all | solution.py:12
  67.0 53.5 %all-gather.4.cloned.1.call-start = ((), (), s32[]{:S(2)}) async-start(), calls=%async_computation.6 | async-start | bytes 1310720 | tf_op jit(solution)/shard_map/all_gather | solution.py:96
Sparse Core Ops, SparseCore 0:
  38.6 39.4 reduce-scatter.1
  80.2 31.6 all-gather.3

commit v12 on v9

--- a/solution.py
+++ b/solution.py
@@ -74,10 +74,9 @@
     down_w = down_w.reshape(holders, rank, feat_width)
 
     base_bf = base_product(hidden_rows, base_weight)
-    base_total = lax.psum_scatter(base_bf, MP, scatter_dimension=1, tiled=True).astype(
-        jnp.float32
-    )
+    base_total = lax.psum_scatter(base_bf, MP, scatter_dimension=1, tiled=True)
     up_w, base_total = lax.optimization_barrier((up_w, base_total))
+    base_total = base_total.astype(jnp.float32)
     for axis in reversed(DP[:-1]):
         up_w = lax.all_gather(up_w, axis, axis=0, tiled=False)
     up_w = up_w.reshape(holders, rank, out_width)

time: 124 us -> 124 us (level)
  transfers between devices with their start and end apart: 3 -> 3, of which waited for: 1 -> 1; matrix products, arithmetic and copies ran while one was open for 5% -> 4% of each run, Pallas kernels for 0% -> 0%
where the time goes in v12:
time: 124 us
  blocking collectives  57.4 us (46%)
  waiting for transfers between devices  33 us (27%)
  between operations  13.5 us (11%)
  Pallas kernels  6.22 us (5%)
  starting transfers between devices  4.51 us (4%)
  matrix products  4.03 us (3%)
  local copies, waits for them, and re-layouts  3.9 us (3%)
    reduce_scatter x1, waiting for transfers between devices, per_device(): base_total = lax.psum_scatter(base_bf, MP, scatter_dimension=1, tiled=True)  33 us
    all_to_all x2, blocking collectives, spread_over(): lax.all_to_all(jnp.broadcast_to(block[None], (n,) + block.shape), axis, 0...  28.8 us
    all_gather x1, blocking collectives, per_device(): both = lax.all_gather(both, DP[-1], axis=0, tiled=False)  28.5 us
    pallas_call x1, Pallas kernels, base_product(): pl.pallas_call(_product_block, grid=(cols // block,), in_specs=[pl.BlockS...  6.22 us
    all_to_all x1, starting transfers between devices, spread_over(): lax.all_to_all(jnp.broadcast_to(block[None], (n,) + block.shape), axis, 0...  4.51 us
    dot_general x1, matrix products, per_device(): jnp.dot(placed.reshape(row_count, holders * rank), up_w.reshape(holders *...  2.69 us
  transfers between devices with their start and end apart: 3, of which 1 were waited for; matrix products, arithmetic and copies ran while one was open for 4% of the time, Pallas kernels for 0%

profile of v12, /device:TPU:1, one launch (start us, length us, event | category | flops | bytes accessed | tf_op | source)
XLA Modules:
  0.0 123.6 jit_solution(13786785032184733111)
XLA Ops:
  6.5 0.0 reduce-scatter.2.cloned.1.call-start
  6.5 6.2 %shard_map.64 = bf16[512,4096]{1,0:T(8,128)(2,1)} custom-call(bf16[512,512]{1,0:T(8,128)(2,1)} %x_ref.1, bf16[512,4096]{1,0:T(8,128)(2,1)} %w_ref.1), custom_call_target="tpu_custom_call" | custom-call | flops 2147483648 | bytes 8912896 | tf_op jit(solution)/shard_map/pallas_call | solution.py:25
  12.8 0.0 copy-start.1
  12.8 0.0 copy-start.2
  12.8 0.0 reduce-scatter.2.cloned.1.call-update
  12.8 0.8 copy-done.1
  13.6 0.0 copy-done.2
  13.6 28.5 %all-gather = bf16[512,768]{1,0:T(8,128)(2,1)S(1)} all-gather(bf16[64,768]{1,0:T(8,128)(2,1)S(1)} %pad_maximum_fusion), channel_id=2, replica_groups=mesh['dp0'=4,'dp2'=8,'mp1'=8,'mp3'=2] {'dp2'}, dimensions={0}, use_global_device_ids=true | all-gather | bytes 884736 | tf_op jit(solution)/shard_map/all_gather | solution.py:69
  42.2 1.6 %broadcast_in_dim.74 = bf16[4,8,1,64,512]{4,3,2,1,0:T(8,128)(2,1)} broadcast(bf16[8,64,512]{2,1,0:T(8,128)(2,1)S(1)} %slice_bitcast_fusion), dimensions={1,3,4} | broadcast | bytes 2621440 | tf_op jit(solution)/shard_map/broadcast_in_dim | solution.py:12
  43.8 0.0 copy-start.3
  43.8 0.0 copy-start.4
  43.8 0.0 copy-start
  43.8 4.5 %all-to-all-start = ((bf16[4,8,1,64,512]{4,3,2,1,0:T(8,128)(2,1)}), bf16[4,8,1,64,512]{4,3,2,1,0:T(8,128)(2,1)S(1)}, u32[]{:S(2)}, u32[]{:S(2)}) async-start(bf16[4,8,1,64,512]{4,3,2,1,0:T(8,128)(2,1)} %broadcast_in_dim.74), calls=%async_computation.1 | async-start | bytes 4194304 | tf_op jit(solution)/shard_map/all_to_all | solution.py:12
  48.3 0.0 all-gather.4.cloned.1.call-start
  48.3 0.7 slice.8
  49.0 0.0 copy-done.3
  49.0 0.0 copy-done.4
  49.0 0.1 select_reduce_fusion.1
  49.1 33.0 %reduce-scatter.2.cloned.1.call-done = bf16[512,256]{1,0:T(8,128)(2,1)} async-done(((bf16[512,4096]{1,0:T(8,128)(2,1)}), bf16[512,256]{1,0:T(8,128)(2,1)}) %reduce-scatter.2.cloned.1.call-update) | async-done | bytes 262160 | tf_op jit(solution)/shard_map/reduce_scatter | solution.py:77
  82.1 0.0 all-gather.4.cloned.1.call-update
  82.1 0.0 all-to-all-done
  82.1 0.0 copy-done
  82.1 1.3 %fusion.3 = f32[2048,512]{1,0:T(8,128)S(1)} fusion(bf16[512,2048]{0,1:T(8,128)(2,1)S(1)} %bitcast.22, bf16[512,512]{1,0:T(8,128)(2,1)S(1)} %copy-done), kind=kOutput, calls=%fused_computation.11 | convolution fusion | flops 1073741824 | bytes 6815744 | tf_op jit(solution)/shard_map/dot_general | solution.py:84
  83.5 0.6 select_reduce_fusion
  84.2 22.2 %all_to_all.15 = bf16[8,1,512,64]{2,3,1,0:T(8,128)(2,1)S(1)} all-to-all(bf16[8,1,512,64]{2,3,1,0:T(8,128)(2,1)S(1)} %broadcast_in_dim.76), channel_id=1, replica_groups=mesh['dp0'=4,'dp2'=8,'mp1'=8,'mp3'=2] {'mp1'}, dimensions={0} | all-to-all | bytes 1048576 | tf_op jit(solution)/shard_map/all_to_all | solution.py:12
  106.4 0.1 broadcast_in_dim.78
  106.5 6.6 %all_to_all.16 = bf16[2,8,1,512,64]{3,4,2,1,0:T(8,128)(2,1)S(1)} all-to-all(bf16[2,8,1,512,64]{3,4,2,1,0:T(8,128)(2,1)S(1)} %broadcast_in_dim.78), channel_id=1, replica_groups=mesh['dp0'=4,'dp2'=8,'mp1'=8,'mp3'=2] {'mp3'}, dimensions={0} | all-to-all | bytes 2097152 | tf_op jit(solution)/shard_map/all_to_all | solution.py:12
  113.1 0.0 copy-start.5
  113.1 0.1 reduce_sum.32
  113.2 0.1 broadcast_select_fusion
  113.4 0.0 all-gather.4.cloned.1.call-done
  113.4 0.6 copy-done.5
  114.0 2.7 %fusion.2 = bf16[512,256]{1,0:T(8,128)(2,1)} fusion(bf16[512,2048]{0,1:T(8,128)(2,1)S(1)} %bitcast.26, bf16[2048,256]{1,0:T(8,128)(2,1)} %bitcast.30, bf16[512,256]{1,0:T(8,128)(2,1)S(1)} %copy-done.5), kind=kOutput, calls=%fused_computation.5 | convolution fusion | flops 537526272 | bytes 3670016 | tf_op jit(solution)/shard_map/dot_general | solution.py:97
  (4 shorter events, 0.1 us)
Async XLA Ops:
  6.5 75.6 %reduce-scatter.2.cloned.1.call-start = ((), (), s32[]{:S(2)}) async-start(), calls=%async_computation.4 | async-start | bytes 4456448 | tf_op jit(solution)/shard_map/reduce_scatter | solution.py:77
  12.8 0.8 copy-start.1
  12.8 0.8 copy-start.2
  43.8 5.2 %copy-start.3 = (s32[512,1]{0,1:T(1,128)S(1)}, s32[512,1]{0,1:T(1,128)}, u32[]{:S(2)}) copy-start(s32[512,1]{0,1:T(1,128)} %param.10) | copy-start | bytes 6148
  43.8 5.2 %copy-start.4 = (s32[32]{0:T(128)S(1)}, s32[32]{0:T(128)}, u32[]{:S(2)}) copy-start(s32[32]{0:T(128)} %param.11) | copy-start | bytes 388
  43.8 38.4 %copy-start = (bf16[512,512]{1,0:T(8,128)(2,1)S(1)}, bf16[512,512]{1,0:T(8,128)(2,1)}, u32[]{:S(2)}) copy-start(bf16[512,512]{1,0:T(8,128)(2,1)} %x_ref.1) | copy-start | bytes 1572868
  43.8 38.4 %all-to-all-start = ((bf16[4,8,1,64,512]{4,3,2,1,0:T(8,128)(2,1)}), bf16[4,8,1,64,512]{4,3,2,1,0:T(8,128)(2,1)S(1)}, u32[]{:S(2)}, u32[]{:S(2)}) async-start(bf16[4,8,1,64,512]{4,3,2,1,0:T(8,128)(2,1)} %broadcast_in_dim.74), calls=%async_computation.1 | async-start | bytes 4194304 | tf_op jit(solution)/shard_map/all_to_all | solution.py:12
  48.3 65.1 %all-gather.4.cloned.1.call-start = ((), (), s32[]{:S(2)}) async-start(), calls=%async_computation.5 | async-start | bytes 1310720 | tf_op jit(solution)/shard_map/all_gather | solution.py:81
  113.1 0.9 copy-start.5
Sparse Core Ops, SparseCore 0:
  12.9 69.1 reduce-scatter.1
  84.2 29.0 all-gather.3

commit v13 on v9

--- a/solution.py
+++ b/solution.py
@@ -18,7 +18,7 @@
     )
 
 
-def base_product(x, w, block=1024):
+def base_product(x, w, block=512):
     rows, inner = x.shape
     cols = w.shape[1]
     block = block if cols % block == 0 else cols

time: 124 us -> 127 us (1.024)
  Pallas kernels: 6.28 us -> 8.4 us
    pallas_call x1, Pallas kernels: 6.28 us -> 8.4 us  [base_product(): pl.pallas_call(_product_block, grid=(cols // block,), in_specs=[pl.BlockS...]
where the time goes in v13:
time: 127 us; the launch traced here: 126 us
  blocking collectives  57.4 us (45%)
  waiting for transfers between devices  33 us (26%)
  between operations  13.5 us (11%)
  Pallas kernels  8.4 us (7%)
  starting transfers between devices  4.51 us (4%)
  matrix products  4.03 us (3%)
  local copies, waits for them, and re-layouts  3.29 us (3%)
  other arithmetic  2.02 us (2%)
    reduce_scatter x1, waiting for transfers between devices, per_device(): lax.psum_scatter(base_bf, MP, scatter_dimension=1, tiled=True)  33 us
    all_to_all x2, blocking collectives, spread_over(): lax.all_to_all(jnp.broadcast_to(block[None], (n,) + block.shape), axis, 0...  28.8 us
    all_gather x1, blocking collectives, per_device(): both = lax.all_gather(both, DP[-1], axis=0, tiled=False)  28.5 us
    pallas_call x1, Pallas kernels, base_product(): pl.pallas_call(_product_block, grid=(cols // block,), in_specs=[pl.BlockS...  8.4 us
    all_to_all x1, starting transfers between devices, spread_over(): lax.all_to_all(jnp.broadcast_to(block[None], (n,) + block.shape), axis, 0...  4.5 us
    dot_general x1, matrix products, per_device(): jnp.dot(placed.reshape(row_count, holders * rank), up_w.reshape(holders *...  2.69 us
  transfers between devices with their start and end apart: 3, of which 1 were waited for; matrix products, arithmetic and copies ran while one was open for 5% of the time, Pallas kernels for 0%

profile of v13, /device:TPU:1, one launch (start us, length us, event | category | flops | bytes accessed | tf_op | source)
XLA Modules:
  0.0 126.1 jit_solution(9005727495850626328)
XLA Ops:
  6.5 0.0 reduce-scatter.2.cloned.1.call-start
  6.5 8.4 %shard_map.64 = bf16[512,4096]{1,0:T(8,128)(2,1)} custom-call(bf16[512,512]{1,0:T(8,128)(2,1)} %x_ref.1, bf16[512,4096]{1,0:T(8,128)(2,1)} %w_ref.1), custom_call_target="tpu_custom_call" | custom-call | flops 2147483648 | bytes 8912896 | tf_op jit(solution)/shard_map/pallas_call | solution.py:25
  14.9 0.0 copy-start.1
  14.9 0.0 copy-start.2
  14.9 0.0 reduce-scatter.2.cloned.1.call-update
  15.0 0.8 copy-done.1
  15.8 0.0 copy-done.2
  15.8 28.5 %all-gather = bf16[512,768]{1,0:T(8,128)(2,1)S(1)} all-gather(bf16[64,768]{1,0:T(8,128)(2,1)S(1)} %pad_maximum_fusion), channel_id=2, replica_groups=mesh['dp0'=4,'dp2'=8,'mp1'=8,'mp3'=2] {'dp2'}, dimensions={0}, use_global_device_ids=true | all-gather | bytes 884736 | tf_op jit(solution)/shard_map/all_gather | solution.py:69
  44.4 1.6 %broadcast_in_dim.74 = bf16[4,8,1,64,512]{4,3,2,1,0:T(8,128)(2,1)} broadcast(bf16[8,64,512]{2,1,0:T(8,128)(2,1)S(1)} %slice_bitcast_fusion), dimensions={1,3,4} | broadcast | bytes 2621440 | tf_op jit(solution)/shard_map/broadcast_in_dim | solution.py:12
  45.9 0.0 copy-start.3
  46.0 0.0 copy-start.4
  46.0 0.0 copy-start
  46.0 4.5 %all-to-all-start = ((bf16[4,8,1,64,512]{4,3,2,1,0:T(8,128)(2,1)}), bf16[4,8,1,64,512]{4,3,2,1,0:T(8,128)(2,1)S(1)}, u32[]{:S(2)}, u32[]{:S(2)}) async-start(bf16[4,8,1,64,512]{4,3,2,1,0:T(8,128)(2,1)} %broadcast_in_dim.74), calls=%async_computation.1 | async-start | bytes 4194304 | tf_op jit(solution)/shard_map/all_to_all | solution.py:12
  50.5 0.0 all-gather.4.cloned.1.call-start
  50.5 0.7 slice.8
  51.2 0.0 copy-done.3
  51.2 0.0 copy-done.4
  51.2 0.1 select_reduce_fusion.1
  51.3 33.0 %reduce-scatter.2.cloned.1.call-done = bf16[512,256]{1,0:T(8,128)(2,1)} async-done(((bf16[512,4096]{1,0:T(8,128)(2,1)}), bf16[512,256]{1,0:T(8,128)(2,1)}) %reduce-scatter.2.cloned.1.call-update) | async-done | bytes 262160 | tf_op jit(solution)/shard_map/reduce_scatter | solution.py:77
  84.3 1.0 convert_element_type.21
  85.3 0.0 all-gather.4.cloned.1.call-update
  85.3 0.0 all-to-all-done
  85.3 0.0 copy-done
  85.3 1.3 %fusion.3 = f32[2048,512]{1,0:T(8,128)S(1)} fusion(bf16[512,2048]{0,1:T(8,128)(2,1)S(1)} %bitcast.22, bf16[512,512]{1,0:T(8,128)(2,1)S(1)} %copy-done), kind=kOutput, calls=%fused_computation.11 | convolution fusion | flops 1073741824 | bytes 6815744 | tf_op jit(solution)/shard_map/dot_general | solution.py:85
  86.7 0.6 select_reduce_fusion
  87.3 22.2 %all_to_all.15 = bf16[8,1,512,64]{2,3,1,0:T(8,128)(2,1)S(1)} all-to-all(bf16[8,1,512,64]{2,3,1,0:T(8,128)(2,1)S(1)} %broadcast_in_dim.76), channel_id=1, replica_groups=mesh['dp0'=4,'dp2'=8,'mp1'=8,'mp3'=2] {'mp1'}, dimensions={0} | all-to-all | bytes 1048576 | tf_op jit(solution)/shard_map/all_to_all | solution.py:12
  109.6 0.1 broadcast_in_dim.78
  109.7 6.6 %all_to_all.16 = bf16[2,8,1,512,64]{3,4,2,1,0:T(8,128)(2,1)S(1)} all-to-all(bf16[2,8,1,512,64]{3,4,2,1,0:T(8,128)(2,1)S(1)} %broadcast_in_dim.78), channel_id=1, replica_groups=mesh['dp0'=4,'dp2'=8,'mp1'=8,'mp3'=2] {'mp3'}, dimensions={0} | all-to-all | bytes 2097152 | tf_op jit(solution)/shard_map/all_to_all | solution.py:12
  116.3 0.1 reduce_sum.32
  116.4 0.1 broadcast_select_fusion
  116.6 0.0 all-gather.4.cloned.1.call-done
  116.6 2.7 %fusion.2 = bf16[512,256]{1,0:T(8,128)(2,1)} fusion(f32[512,256]{1,0:T(8,128)S(1)} %convert_element_type.21, bf16[512,2048]{0,1:T(8,128)(2,1)S(1)} %bitcast.26, bf16[2048,256]{1,0:T(8,128)(2,1)} %bitcast.30), kind=kOutput, calls=%fused_computation.5 | convolution fusion | flops 537395200 | bytes 3932160 | tf_op jit(solution)/shard_map/dot_general | solution.py:98
  (4 shorter events, 0.1 us)
Async XLA Ops:
  6.5 77.7 %reduce-scatter.2.cloned.1.call-start = ((), (), s32[]{:S(2)}) async-start(), calls=%async_computation.4 | async-start | bytes 4456448 | tf_op jit(solution)/shard_map/reduce_scatter | solution.py:77
  14.9 0.8 copy-start.1
  14.9 0.8 copy-start.2
  45.9 5.2 %copy-start.3 = (s32[512,1]{0,1:T(1,128)S(1)}, s32[512,1]{0,1:T(1,128)}, u32[]{:S(2)}) copy-start(s32[512,1]{0,1:T(1,128)} %param.10) | copy-start | bytes 6148
  46.0 5.2 %copy-start.4 = (s32[32]{0:T(128)S(1)}, s32[32]{0:T(128)}, u32[]{:S(2)}) copy-start(s32[32]{0:T(128)} %param.11) | copy-start | bytes 388
  46.0 39.4 %copy-start = (bf16[512,512]{1,0:T(8,128)(2,1)S(1)}, bf16[512,512]{1,0:T(8,128)(2,1)}, u32[]{:S(2)}) copy-start(bf16[512,512]{1,0:T(8,128)(2,1)} %x_ref.1) | copy-start | bytes 1572868
  46.0 39.3 %all-to-all-start = ((bf16[4,8,1,64,512]{4,3,2,1,0:T(8,128)(2,1)}), bf16[4,8,1,64,512]{4,3,2,1,0:T(8,128)(2,1)S(1)}, u32[]{:S(2)}, u32[]{:S(2)}) async-start(bf16[4,8,1,64,512]{4,3,2,1,0:T(8,128)(2,1)} %broadcast_in_dim.74), calls=%async_computation.1 | async-start | bytes 4194304 | tf_op jit(solution)/shard_map/all_to_all | solution.py:12
  50.5 66.1 %all-gather.4.cloned.1.call-start = ((), (), s32[]{:S(2)}) async-start(), calls=%async_computation.5 | async-start | bytes 1310720 | tf_op jit(solution)/shard_map/all_gather | solution.py:82
Sparse Core Ops, SparseCore 0:
  15.1 69.1 reduce-scatter.1
  86.4 29.1 all-gather.3

commit v14 on v13

--- a/solution.py
+++ b/solution.py
@@ -18,7 +18,7 @@
     )
 
 
-def base_product(x, w, block=512):
+def base_product(x, w, block=2048):
     rows, inner = x.shape
     cols = w.shape[1]
     block = block if cols % block == 0 else cols

time: 127 us -> 124 us (0.976)
  Pallas kernels: 8.4 us -> 5.55 us
    pallas_call x1, Pallas kernels: 8.4 us -> 5.55 us  [base_product(): pl.pallas_call(_product_block, grid=(cols // block,), in_specs=[pl.BlockS...]
where the time goes in v14:
time: 124 us; the launch traced here: 123 us
  blocking collectives  57.4 us (46%)
  waiting for transfers between devices  33 us (27%)
  between operations  13.5 us (11%)
  Pallas kernels  5.55 us (4%)
  starting transfers between devices  4.51 us (4%)
  matrix products  4.03 us (3%)
  local copies, waits for them, and re-layouts  3.29 us (3%)
  other arithmetic  2.02 us (2%)
    reduce_scatter x1, waiting for transfers between devices, per_device(): lax.psum_scatter(base_bf, MP, scatter_dimension=1, tiled=True)  33 us
    all_to_all x2, blocking collectives, spread_over(): lax.all_to_all(jnp.broadcast_to(block[None], (n,) + block.shape), axis, 0...  28.8 us
    all_gather x1, blocking collectives, per_device(): both = lax.all_gather(both, DP[-1], axis=0, tiled=False)  28.6 us
    pallas_call x1, Pallas kernels, base_product(): pl.pallas_call(_product_block, grid=(cols // block,), in_specs=[pl.BlockS...  5.55 us
    all_to_all x1, starting transfers between devices, spread_over(): lax.all_to_all(jnp.broadcast_to(block[None], (n,) + block.shape), axis, 0...  4.5 us
    dot_general x1, matrix products, per_device(): jnp.dot(placed.reshape(row_count, holders * rank), up_w.reshape(holders *...  2.68 us
  transfers between devices with their start and end apart: 3, of which 1 were waited for; matrix products, arithmetic and copies ran while one was open for 5% of the time, Pallas kernels for 0%

profile of v14, /device:TPU:1, one launch (start us, length us, event | category | flops | bytes accessed | tf_op | source)
XLA Modules:
  0.0 123.3 jit_solution(14012004752849235025)
XLA Ops:
  6.5 0.0 reduce-scatter.2.cloned.1.call-start
  6.5 5.5 %shard_map.64 = bf16[512,4096]{1,0:T(8,128)(2,1)} custom-call(bf16[512,512]{1,0:T(8,128)(2,1)} %x_ref.1, bf16[512,4096]{1,0:T(8,128)(2,1)} %w_ref.1), custom_call_target="tpu_custom_call" | custom-call | flops 2147483648 | bytes 8912896 | tf_op jit(solution)/shard_map/pallas_call | solution.py:25
  12.1 0.0 copy-start.1
  12.1 0.0 copy-start.2
  12.1 0.0 reduce-scatter.2.cloned.1.call-update
  12.1 0.8 copy-done.1
  12.9 0.0 copy-done.2
  12.9 28.6 %all-gather = bf16[512,768]{1,0:T(8,128)(2,1)S(1)} all-gather(bf16[64,768]{1,0:T(8,128)(2,1)S(1)} %pad_maximum_fusion), channel_id=2, replica_groups=mesh['dp0'=4,'dp2'=8,'mp1'=8,'mp3'=2] {'dp2'}, dimensions={0}, use_global_device_ids=true | all-gather | bytes 884736 | tf_op jit(solution)/shard_map/all_gather | solution.py:69
  41.5 1.6 %broadcast_in_dim.74 = bf16[4,8,1,64,512]{4,3,2,1,0:T(8,128)(2,1)} broadcast(bf16[8,64,512]{2,1,0:T(8,128)(2,1)S(1)} %slice_bitcast_fusion), dimensions={1,3,4} | broadcast | bytes 2621440 | tf_op jit(solution)/shard_map/broadcast_in_dim | solution.py:12
  43.1 0.0 copy-start.3
  43.1 0.0 copy-start.4
  43.1 0.0 copy-start
  43.1 4.5 %all-to-all-start = ((bf16[4,8,1,64,512]{4,3,2,1,0:T(8,128)(2,1)}), bf16[4,8,1,64,512]{4,3,2,1,0:T(8,128)(2,1)S(1)}, u32[]{:S(2)}, u32[]{:S(2)}) async-start(bf16[4,8,1,64,512]{4,3,2,1,0:T(8,128)(2,1)} %broadcast_in_dim.74), calls=%async_computation.1 | async-start | bytes 4194304 | tf_op jit(solution)/shard_map/all_to_all | solution.py:12
  47.6 0.0 all-gather.4.cloned.1.call-start
  47.6 0.7 slice.8
  48.3 0.0 copy-done.3
  48.3 0.0 copy-done.4
  48.3 0.1 select_reduce_fusion.1
  48.5 33.0 %reduce-scatter.2.cloned.1.call-done = bf16[512,256]{1,0:T(8,128)(2,1)} async-done(((bf16[512,4096]{1,0:T(8,128)(2,1)}), bf16[512,256]{1,0:T(8,128)(2,1)}) %reduce-scatter.2.cloned.1.call-update) | async-done | bytes 262160 | tf_op jit(solution)/shard_map/reduce_scatter | solution.py:77
  81.4 1.0 convert_element_type.21
  82.4 0.0 all-gather.4.cloned.1.call-update
  82.4 0.0 all-to-all-done
  82.5 0.0 copy-done
  82.5 1.3 %fusion.3 = f32[2048,512]{1,0:T(8,128)S(1)} fusion(bf16[512,2048]{0,1:T(8,128)(2,1)S(1)} %bitcast.22, bf16[512,512]{1,0:T(8,128)(2,1)S(1)} %copy-done), kind=kOutput, calls=%fused_computation.11 | convolution fusion | flops 1073741824 | bytes 6815744 | tf_op jit(solution)/shard_map/dot_general | solution.py:85
  83.8 0.6 select_reduce_fusion
  84.5 22.2 %all_to_all.15 = bf16[8,1,512,64]{2,3,1,0:T(8,128)(2,1)S(1)} all-to-all(bf16[8,1,512,64]{2,3,1,0:T(8,128)(2,1)S(1)} %broadcast_in_dim.76), channel_id=1, replica_groups=mesh['dp0'=4,'dp2'=8,'mp1'=8,'mp3'=2] {'mp1'}, dimensions={0} | all-to-all | bytes 1048576 | tf_op jit(solution)/shard_map/all_to_all | solution.py:12
  106.7 0.1 broadcast_in_dim.78
  106.8 6.6 %all_to_all.16 = bf16[2,8,1,512,64]{3,4,2,1,0:T(8,128)(2,1)S(1)} all-to-all(bf16[2,8,1,512,64]{3,4,2,1,0:T(8,128)(2,1)S(1)} %broadcast_in_dim.78), channel_id=1, replica_groups=mesh['dp0'=4,'dp2'=8,'mp1'=8,'mp3'=2] {'mp3'}, dimensions={0} | all-to-all | bytes 2097152 | tf_op jit(solution)/shard_map/all_to_all | solution.py:12
  113.4 0.1 reduce_sum.32
  113.6 0.1 broadcast_select_fusion
  113.7 0.0 all-gather.4.cloned.1.call-done
  113.7 2.7 %fusion.2 = bf16[512,256]{1,0:T(8,128)(2,1)} fusion(f32[512,256]{1,0:T(8,128)S(1)} %convert_element_type.21, bf16[512,2048]{0,1:T(8,128)(2,1)S(1)} %bitcast.26, bf16[2048,256]{1,0:T(8,128)(2,1)} %bitcast.30), kind=kOutput, calls=%fused_computation.5 | convolution fusion | flops 537395200 | bytes 3932160 | tf_op jit(solution)/shard_map/dot_general | solution.py:98
  (4 shorter events, 0.1 us)
Async XLA Ops:
  6.5 74.9 %reduce-scatter.2.cloned.1.call-start = ((), (), s32[]{:S(2)}) async-start(), calls=%async_computation.4 | async-start | bytes 4456448 | tf_op jit(solution)/shard_map/reduce_scatter | solution.py:77
  12.1 0.8 copy-start.1
  12.1 0.8 copy-start.2
  43.1 5.2 %copy-start.3 = (s32[512,1]{0,1:T(1,128)S(1)}, s32[512,1]{0,1:T(1,128)}, u32[]{:S(2)}) copy-start(s32[512,1]{0,1:T(1,128)} %param.10) | copy-start | bytes 6148
  43.1 5.2 %copy-start.4 = (s32[32]{0:T(128)S(1)}, s32[32]{0:T(128)}, u32[]{:S(2)}) copy-start(s32[32]{0:T(128)} %param.11) | copy-start | bytes 388
  43.1 39.3 %copy-start = (bf16[512,512]{1,0:T(8,128)(2,1)S(1)}, bf16[512,512]{1,0:T(8,128)(2,1)}, u32[]{:S(2)}) copy-start(bf16[512,512]{1,0:T(8,128)(2,1)} %x_ref.1) | copy-start | bytes 1572868
  43.1 39.3 %all-to-all-start = ((bf16[4,8,1,64,512]{4,3,2,1,0:T(8,128)(2,1)}), bf16[4,8,1,64,512]{4,3,2,1,0:T(8,128)(2,1)S(1)}, u32[]{:S(2)}, u32[]{:S(2)}) async-start(bf16[4,8,1,64,512]{4,3,2,1,0:T(8,128)(2,1)} %broadcast_in_dim.74), calls=%async_computation.1 | async-start | bytes 4194304 | tf_op jit(solution)/shard_map/all_to_all | solution.py:12
  47.6 66.1 %all-gather.4.cloned.1.call-start = ((), (), s32[]{:S(2)}) async-start(), calls=%async_computation.5 | async-start | bytes 1310720 | tf_op jit(solution)/shard_map/all_gather | solution.py:82
Sparse Core Ops, SparseCore 0:
  12.2 69.1 reduce-scatter.1
  83.5 29.0 all-gather.3

commit v15 on v14

--- a/solution.py
+++ b/solution.py
@@ -18,7 +18,7 @@
     )
 
 
-def base_product(x, w, block=2048):
+def base_product(x, w, block=4096):
     rows, inner = x.shape
     cols = w.shape[1]
     block = block if cols % block == 0 else cols

time: 124 us -> 125 us (level)
  no operation moved by 1% of the time
where the time goes in v15:
time: 125 us; the launch traced here: 124 us
  blocking collectives  57.4 us (46%)
  waiting for transfers between devices  33 us (26%)
  between operations  13.5 us (11%)
  Pallas kernels  6.64 us (5%)
  starting transfers between devices  4.51 us (4%)
  matrix products  4.03 us (3%)
  local copies, waits for them, and re-layouts  3.29 us (3%)
  other arithmetic  2.02 us (2%)
    reduce_scatter x1, waiting for transfers between devices, per_device(): lax.psum_scatter(base_bf, MP, scatter_dimension=1, tiled=True)  33 us
    all_to_all x2, blocking collectives, spread_over(): lax.all_to_all(jnp.broadcast_to(block[None], (n,) + block.shape), axis, 0...  28.8 us
    all_gather x1, blocking collectives, per_device(): both = lax.all_gather(both, DP[-1], axis=0, tiled=False)  28.6 us
    pallas_call x1, Pallas kernels, base_product(): pl.pallas_call(_product_block, grid=(cols // block,), in_specs=[pl.BlockS...  6.64 us
    all_to_all x1, starting transfers between devices, spread_over(): lax.all_to_all(jnp.broadcast_to(block[None], (n,) + block.shape), axis, 0...  4.5 us
    dot_general x1, matrix products, per_device(): jnp.dot(placed.reshape(row_count, holders * rank), up_w.reshape(holders *...  2.68 us
  transfers between devices with their start and end apart: 3, of which 1 were waited for; matrix products, arithmetic and copies ran while one was open for 5% of the time, Pallas kernels for 0%

profile of v15, /device:TPU:1, one launch (start us, length us, event | category | flops | bytes accessed | tf_op | source)
XLA Modules:
  0.0 124.3 jit_solution(11679361658102160350)
XLA Ops:
  6.5 0.0 reduce-scatter.2.cloned.1.call-start
  6.5 6.6 %shard_map.64 = bf16[512,4096]{1,0:T(8,128)(2,1)} custom-call(bf16[512,512]{1,0:T(8,128)(2,1)} %x_ref.1, bf16[512,4096]{1,0:T(8,128)(2,1)} %w_ref.1), custom_call_target="tpu_custom_call" | custom-call | flops 2147483648 | bytes 8912896 | tf_op jit(solution)/shard_map/pallas_call | solution.py:25
  13.2 0.0 copy-start.1
  13.2 0.0 copy-start.2
  13.2 0.0 reduce-scatter.2.cloned.1.call-update
  13.2 0.8 copy-done.1
  14.0 0.0 copy-done.2
  14.0 28.6 %all-gather = bf16[512,768]{1,0:T(8,128)(2,1)S(1)} all-gather(bf16[64,768]{1,0:T(8,128)(2,1)S(1)} %pad_maximum_fusion), channel_id=2, replica_groups=mesh['dp0'=4,'dp2'=8,'mp1'=8,'mp3'=2] {'dp2'}, dimensions={0}, use_global_device_ids=true | all-gather | bytes 884736 | tf_op jit(solution)/shard_map/all_gather | solution.py:69
  42.6 1.6 %broadcast_in_dim.74 = bf16[4,8,1,64,512]{4,3,2,1,0:T(8,128)(2,1)} broadcast(bf16[8,64,512]{2,1,0:T(8,128)(2,1)S(1)} %slice_bitcast_fusion), dimensions={1,3,4} | broadcast | bytes 2621440 | tf_op jit(solution)/shard_map/broadcast_in_dim | solution.py:12
  44.2 0.0 copy-start.3
  44.2 0.0 copy-start.4
  44.2 0.0 copy-start
  44.2 4.5 %all-to-all-start = ((bf16[4,8,1,64,512]{4,3,2,1,0:T(8,128)(2,1)}), bf16[4,8,1,64,512]{4,3,2,1,0:T(8,128)(2,1)S(1)}, u32[]{:S(2)}, u32[]{:S(2)}) async-start(bf16[4,8,1,64,512]{4,3,2,1,0:T(8,128)(2,1)} %broadcast_in_dim.74), calls=%async_computation.1 | async-start | bytes 4194304 | tf_op jit(solution)/shard_map/all_to_all | solution.py:12
  48.7 0.0 all-gather.4.cloned.1.call-start
  48.7 0.7 slice.8
  49.4 0.0 copy-done.3
  49.4 0.0 copy-done.4
  49.4 0.1 select_reduce_fusion.1
  49.5 33.0 %reduce-scatter.2.cloned.1.call-done = bf16[512,256]{1,0:T(8,128)(2,1)} async-done(((bf16[512,4096]{1,0:T(8,128)(2,1)}), bf16[512,256]{1,0:T(8,128)(2,1)}) %reduce-scatter.2.cloned.1.call-update) | async-done | bytes 262160 | tf_op jit(solution)/shard_map/reduce_scatter | solution.py:77
  82.5 1.0 convert_element_type.21
  83.5 0.0 all-gather.4.cloned.1.call-update
  83.5 0.0 all-to-all-done
  83.5 0.0 copy-done
  83.5 1.3 %fusion.3 = f32[2048,512]{1,0:T(8,128)S(1)} fusion(bf16[512,2048]{0,1:T(8,128)(2,1)S(1)} %bitcast.22, bf16[512,512]{1,0:T(8,128)(2,1)S(1)} %copy-done), kind=kOutput, calls=%fused_computation.11 | convolution fusion | flops 1073741824 | bytes 6815744 | tf_op jit(solution)/shard_map/dot_general | solution.py:85
  84.9 0.6 select_reduce_fusion
  85.6 22.2 %all_to_all.15 = bf16[8,1,512,64]{2,3,1,0:T(8,128)(2,1)S(1)} all-to-all(bf16[8,1,512,64]{2,3,1,0:T(8,128)(2,1)S(1)} %broadcast_in_dim.76), channel_id=1, replica_groups=mesh['dp0'=4,'dp2'=8,'mp1'=8,'mp3'=2] {'mp1'}, dimensions={0} | all-to-all | bytes 1048576 | tf_op jit(solution)/shard_map/all_to_all | solution.py:12
  107.8 0.1 broadcast_in_dim.78
  107.9 6.6 %all_to_all.16 = bf16[2,8,1,512,64]{3,4,2,1,0:T(8,128)(2,1)S(1)} all-to-all(bf16[2,8,1,512,64]{3,4,2,1,0:T(8,128)(2,1)S(1)} %broadcast_in_dim.78), channel_id=1, replica_groups=mesh['dp0'=4,'dp2'=8,'mp1'=8,'mp3'=2] {'mp3'}, dimensions={0} | all-to-all | bytes 2097152 | tf_op jit(solution)/shard_map/all_to_all | solution.py:12
  114.5 0.1 reduce_sum.32
  114.6 0.1 broadcast_select_fusion
  114.8 0.0 all-gather.4.cloned.1.call-done
  114.8 2.7 %fusion.2 = bf16[512,256]{1,0:T(8,128)(2,1)} fusion(f32[512,256]{1,0:T(8,128)S(1)} %convert_element_type.21, bf16[512,2048]{0,1:T(8,128)(2,1)S(1)} %bitcast.26, bf16[2048,256]{1,0:T(8,128)(2,1)} %bitcast.30), kind=kOutput, calls=%fused_computation.5 | convolution fusion | flops 537395200 | bytes 3932160 | tf_op jit(solution)/shard_map/dot_general | solution.py:98
  (4 shorter events, 0.1 us)
Async XLA Ops:
  6.5 76.0 %reduce-scatter.2.cloned.1.call-start = ((), (), s32[]{:S(2)}) async-start(), calls=%async_computation.4 | async-start | bytes 4456448 | tf_op jit(solution)/shard_map/reduce_scatter | solution.py:77
  13.2 0.8 copy-start.1
  13.2 0.8 copy-start.2
  44.2 5.2 %copy-start.3 = (s32[512,1]{0,1:T(1,128)S(1)}, s32[512,1]{0,1:T(1,128)}, u32[]{:S(2)}) copy-start(s32[512,1]{0,1:T(1,128)} %param.10) | copy-start | bytes 6148
  44.2 5.2 %copy-start.4 = (s32[32]{0:T(128)S(1)}, s32[32]{0:T(128)}, u32[]{:S(2)}) copy-start(s32[32]{0:T(128)} %param.11) | copy-start | bytes 388
  44.2 39.3 %copy-start = (bf16[512,512]{1,0:T(8,128)(2,1)S(1)}, bf16[512,512]{1,0:T(8,128)(2,1)}, u32[]{:S(2)}) copy-start(bf16[512,512]{1,0:T(8,128)(2,1)} %x_ref.1) | copy-start | bytes 1572868
  44.2 39.3 %all-to-all-start = ((bf16[4,8,1,64,512]{4,3,2,1,0:T(8,128)(2,1)}), bf16[4,8,1,64,512]{4,3,2,1,0:T(8,128)(2,1)S(1)}, u32[]{:S(2)}, u32[]{:S(2)}) async-start(bf16[4,8,1,64,512]{4,3,2,1,0:T(8,128)(2,1)} %broadcast_in_dim.74), calls=%async_computation.1 | async-start | bytes 4194304 | tf_op jit(solution)/shard_map/all_to_all | solution.py:12
  48.7 66.1 %all-gather.4.cloned.1.call-start = ((), (), s32[]{:S(2)}) async-start(), calls=%async_computation.5 | async-start | bytes 1310720 | tf_op jit(solution)/shard_map/all_gather | solution.py:82
Sparse Core Ops, SparseCore 0:
  13.3 69.1 reduce-scatter.1
  84.6 29.0 all-gather.3
